TPU v7x, 32 devices: a whole 2x2x4 slice. The times are simulated.
32 devices in a mesh: blk: 8 (over z, y), grp: 4 (over x, core).
Axes of the slice: x: 2, y: 2, z: 4, core: 2. Of those that a mesh axis runs over, the one named last changes fastest.
Arguments:
- state: float32 [2, 128, 4096], P(None, None, ('blk', 'grp')), may hold values from -3 to 3
- prev_slope: float32 [2, 128, 4096], P(None, None, ('blk', 'grp')), may hold values from -4 to 4
- positions: float32 [2, 4096], P(None, ('blk', 'grp')), may hold values from -1 to 1
- pump: float32 [4096], P(('blk', 'grp')), may hold values from -0.5 to 1.5
- detuning: float32 [4096], P(('blk', 'grp')), may hold values from -4 to 4
- kappa: float32 [6, 4096], P(None, ('blk', 'grp')), may hold values from 0.2 to 1
- neighbours: int32 [6, 4096], P(None, ('blk', 'grp')), may hold values from 0 to 255
- send_list: int32 [2, 2048], P(None, ('blk', 'grp')), may hold values from 0 to 127
Outputs:
- slope: float32 [2, 128, 4096], P(None, None, ('blk', 'grp'))
Inputs may be any that keep to these rules, and one draw needn't show every extreme that they name: `neighbours`: places below 128 are the block's own emitters, the next 64 those listed by the previous block, the last 64 those listed by the next block. `send_list`: places in the listing block.
All inputs are finite; a program needn't handle non-finite values.
Results may differ from a plain program's by a relative error of at most 0.0012.
Values may be sent and summed in bfloat16 or wider, within the bound.
No kernel may reach another device: no remote copies, remote signals or barrier semaphores. Data moves between devices by JAX's collectives and lax.ppermute only.
A program may use at most 64 MiB of HBM per device.

v0:
```python
import math

import jax
import jax.numpy as jnp
from jax import lax
from jax.sharding import PartitionSpec as P

section_weight = 0.25
phase_rate = 60.0
alpha_factor = 2.0


def from_behind(array, axis, by):
    size = lax.axis_size(axis)
    return lax.ppermute(array, axis, [(i, (i + by) % size) for i in range(size)])


def with_halo(cells, sides, width):
    for axis, dim in sides:
        count = lax.axis_size(axis)
        ends = count - 1
        head = lax.slice_in_dim(cells, 0, width, axis=dim)
        tail = lax.slice_in_dim(cells, cells.shape[dim] - width, cells.shape[dim], axis=dim)
        cells = jnp.concatenate(
            [
                lax.ppermute(tail, axis, [(i, (i + 1) % count) for i in range(ends)]),
                cells,
                lax.ppermute(head, axis, [((i + 1) % count, i) for i in range(ends)]),
            ],
            axis=dim,
        )
    return cells


def kernel_table(source_place, target_place, scaled):
    horizontal = target_place[0][None, :] - source_place[0][:, None]
    vertical = target_place[1][None, :] - source_place[1][:, None]
    phase = phase_rate * (horizontal * horizontal + vertical * vertical)
    cosine = (scaled * jnp.cos(phase)).astype(jnp.bfloat16)
    sine_part = (scaled * jnp.sin(phase)).astype(jnp.bfloat16)
    return jnp.concatenate([cosine, sine_part], axis=1)


def block_columns(total, fields, source_place, target_place, scaled):
    members = fields.shape[1]
    targets = target_place.shape[1]
    kernel = kernel_table(source_place, target_place, scaled)
    flat = fields.reshape(2 * members, fields.shape[2])
    product = jnp.dot(flat, kernel, preferred_element_type=jnp.float32)
    real_part = product[:members, :targets] - product[members:, targets:]
    imag_part = product[:members, targets:] + product[members:, :targets]
    return total + jnp.stack([real_part, imag_part])


def local(state, prev_slope, positions, pump, detuning, kappa, neighbours, send_list):
    members = state.shape[1]
    rows_here = state.shape[2]
    block_count = lax.axis_size("blk")
    group_size = lax.axis_size("grp")
    scaled = 1.0 / math.sqrt(rows_here * block_count * group_size)
    section_field = state + section_weight * prev_slope
    section_half = section_field.astype(jnp.bfloat16)
    my_index = lax.axis_index("blk")
    target_place = lax.all_gather(positions, "grp", axis=1, tiled=True)
    source_place = lax.all_gather(positions, "blk", axis=1, tiled=True)
    targets = target_place.shape[1]

    def place_of(block_index):
        return lax.dynamic_slice_in_dim(
            source_place, block_index % block_count * rows_here, rows_here, 1
        )

    def add_block(total, fields, block_index):
        return block_columns(total, fields, place_of(block_index), target_place, scaled)

    empty = jnp.zeros((2, members, targets), jnp.float32)

    def forward(carried):
        return from_behind(carried, "blk", 1)

    def advance_both(step, carry):
        total, upward, downward = carry
        upward = forward(upward)
        downward = from_behind(downward, "blk", -1)
        total = add_block(total, upward, my_index - step)
        total = add_block(total, downward, my_index + step)
        return (total, upward, downward)

    total = add_block(empty, section_half, my_index)
    total, upward, downward = lax.fori_loop(
        1, (block_count - 1) // 2 + 1, advance_both, (total, section_half, section_half)
    )
    upward = forward(upward)
    total = add_block(total, upward, my_index - block_count // 2)
    fresnel = lax.psum_scatter(total, "grp", scatter_dimension=2, tiled=True)
    halo_width = send_list.shape[1]
    to_prev = jnp.take(section_field, send_list[1], axis=2)
    to_next = jnp.take(section_field, send_list[0], axis=2)
    padded = with_halo(
        jnp.concatenate([to_prev, to_next], axis=2), ((("blk", "grp"), 2),), halo_width
    )
    local_buffer = jnp.concatenate(
        [section_field, padded[:, :, :halo_width], padded[:, :, 3 * halo_width :]], axis=2
    )
    coupled = jnp.zeros((2, members, rows_here), jnp.float32)
    for neighbour_slot in range(kappa.shape[0]):
        picked = jnp.take(local_buffer, neighbours[neighbour_slot], axis=2)
        coupled = coupled + kappa[neighbour_slot] * picked
    real_field = section_field[0]
    imag_field = section_field[1]
    modulus = real_field * real_field + imag_field * imag_field
    linear_real = pump - modulus
    linear_imag = detuning - alpha_factor * modulus
    local_real = linear_real * real_field - linear_imag * imag_field
    local_imag = linear_real * imag_field + linear_imag * real_field
    slope_real = local_real + fresnel[0] - coupled[1]
    slope_imag = local_imag + fresnel[1] + coupled[0]
    return jnp.stack([slope_real, slope_imag])


def solution(mesh):
    placed = (
        P(None, None, ("blk", "grp")),
        P(None, None, ("blk", "grp")),
        P(None, ("blk", "grp")),
        P(("blk", "grp")),
        P(("blk", "grp")),
        P(None, ("blk", "grp")),
        P(None, ("blk", "grp")),
        P(None, ("blk", "grp")),
    )
    return jax.shard_map(
        local, mesh=mesh, in_specs=placed, out_specs=P(None, None, ("blk", "grp")), check_vma=False
    )
```

profile of v0, /device:TPU:0, one launch (start us, length us, event | category | flops | bytes accessed | tf_op | source)
XLA Modules:
  0.0 103.9 jit_solution(2091515941593772664)
XLA Ops:
  6.5 0.7 copy-done
  7.2 22.3 %all_gather.7 = f32[2,1024]{1,0:T(2,128)S(1)} all-gather(f32[2,128]{1,0:T(2,128)S(1)} %copy-done), channel_id=1, replica_groups=mesh['blk'=8,'grp'=4] {'blk'}, dimensions={1}, use_global_device_ids=true | all-gather | bytes 9216 | tf_op jit(solution)/shard_map/all_gather | solution.py:65
  29.5 5.1 %all_gather.6 = f32[2,512]{1,0:T(2,128)S(1)} all-gather(f32[2,128]{1,0:T(2,128)S(1)} %copy-done), channel_id=1, replica_groups=mesh['blk'=8,'grp'=4] {'grp'}, dimensions={1}, use_global_device_ids=true | all-gather | bytes 5120 | tf_op jit(solution)/shard_map/all_gather | solution.py:64
  34.6 1.0 fusion.32
  35.6 2.2 %multiply_convert_fusion.5 = (bf16[128,512]{1,0:T(8,128)(2,1)S(1)}, bf16[128,512]{1,0:T(8,128)(2,1)S(1)}, bf16[128,512]{1,0:T(8,128)(2,1)S(1)}, bf16[128,512]{1,0:T(8,128)(2,1)S(1)}) fusion(f32[128]{0:T(128)S(1)} %get-tuple-element.286, f32[128]{0:T(128)S(1)} %get-tuple-element.285, f32[512]{0:T(512)S(1)} %bitcast.149, f32[512]{0:T(512)S(1)} %bitcast.148, ...), kind=kLoop, calls=%fused_computation.60 | loop fusion | flops 1310720 | bytes 530432 | tf_op jit(solution)/shard_map/convert_element_type | solution.py:39
  38.5 24.3 %while.19 = (s32[]{:T(128)}, f32[2,128,512]{1,2,0:T(8,128)S(1)}, bf16[2,128,128]{2,1,0:T(8,128)(2,1)S(1)}, bf16[2,128,128]{2,1,0:T(8,128)(2,1)S(1)}, f32[2,512]{...) while((s32[]{:T(128)}, f32[2,128,512]{1,2,0:T(8,128)S(1)}, ...), condition=%wide.region_1.2_spmd, body=%wide.region_0.1_spmd.sunk | while | flops 137363488 | bytes 9329187 | solution.py:90
  38.6 2.0 %collective-permute-start = (bf16[2,128,128]{2,1,0:T(8,128)(2,1)S(1)}, bf16[2,128,128]{2,1,0:T(8,128)(2,1)S(1)}, u32[]{:S(2)}, u32[]{:S(2)}) collective-permute-start(bf16[2,128,128]{2,1,0:T(8,128)(2,1)S(1)} %get-tuple-element.389), channel_id=1, source_target_pairs={{0,4},{4,8},{8,12},{12,16},{16,20},{20,24},{24,28},{28,0},{1,5},{5... | collective-permute-start | bytes 196616 | tf_op jit(solution)/shard_map/while/body/eval_jaxpr/ppermute | solution.py:15
  40.6 2.2 %multiply_convert_fusion.9 = (bf16[128,512]{1,0:T(8,128)(2,1)S(1)}, bf16[128,512]{1,0:T(8,128)(2,1)S(1)}, bf16[128,512]{1,0:T(8,128)(2,1)S(1)}, bf16[128,512]{1,0:T(8,128)(2,1)S(1)}) fusion(f32[128]{0:T(128)S(1)} %get-tuple-element.360, f32[128]{0:T(128)S(1)} %get-tuple-element.361, f32[512]{0:T(512)S(1)} %bitcast.146, f32[512]{0:T(512)S(1)} %bitcast.145, ...), kind=kLoop, calls=%fused_computation.27.clone.1 | loop fusion | flops 1310720 | bytes 530432 | tf_op jit(solution)/shard_map/while/body/eval_jaxpr/convert_element_type | solution.py:39
  43.3 2.4 %collective-permute-done = bf16[2,128,128]{2,1,0:T(8,128)(2,1)S(1)} collective-permute-done((bf16[2,128,128]{2,1,0:T(8,128)(2,1)S(1)}, bf16[2,128,128]{2,1,0:T(8,128)(2,1)S(1)}, u32[]{:S(2)}, u32[]{:S(2)}) %collective-permute-start) | collective-permute-done | bytes 65568 | tf_op jit(solution)/shard_map/while/body/eval_jaxpr/ppermute | solution.py:15
  46.3 0.7 collective-permute-start.1
  47.0 1.4 %collective-permute-start = (bf16[2,128,128]{2,1,0:T(8,128)(2,1)S(1)}, bf16[2,128,128]{2,1,0:T(8,128)(2,1)S(1)}, u32[]{:S(2)}, u32[]{:S(2)}) collective-permute-start(bf16[2,128,128]{2,1,0:T(8,128)(2,1)S(1)} %get-tuple-element.389), channel_id=1, source_target_pairs={{0,4},{4,8},{8,12},{12,16},{16,20},{20,24},{24,28},{28,0},{1,5},{5... | collective-permute-start | bytes 196616 | tf_op jit(solution)/shard_map/while/body/eval_jaxpr/ppermute | solution.py:15
  48.4 2.2 %multiply_convert_fusion.9 = (bf16[128,512]{1,0:T(8,128)(2,1)S(1)}, bf16[128,512]{1,0:T(8,128)(2,1)S(1)}, bf16[128,512]{1,0:T(8,128)(2,1)S(1)}, bf16[128,512]{1,0:T(8,128)(2,1)S(1)}) fusion(f32[128]{0:T(128)S(1)} %get-tuple-element.360, f32[128]{0:T(128)S(1)} %get-tuple-element.361, f32[512]{0:T(512)S(1)} %bitcast.146, f32[512]{0:T(512)S(1)} %bitcast.145, ...), kind=kLoop, calls=%fused_computation.27.clone.1 | loop fusion | flops 1310720 | bytes 530432 | tf_op jit(solution)/shard_map/while/body/eval_jaxpr/convert_element_type | solution.py:39
  51.1 2.9 %collective-permute-done = bf16[2,128,128]{2,1,0:T(8,128)(2,1)S(1)} collective-permute-done((bf16[2,128,128]{2,1,0:T(8,128)(2,1)S(1)}, bf16[2,128,128]{2,1,0:T(8,128)(2,1)S(1)}, u32[]{:S(2)}, u32[]{:S(2)}) %collective-permute-start) | collective-permute-done | bytes 65568 | tf_op jit(solution)/shard_map/while/body/eval_jaxpr/ppermute | solution.py:15
  55.2 1.6 %collective-permute-start = (bf16[2,128,128]{2,1,0:T(8,128)(2,1)S(1)}, bf16[2,128,128]{2,1,0:T(8,128)(2,1)S(1)}, u32[]{:S(2)}, u32[]{:S(2)}) collective-permute-start(bf16[2,128,128]{2,1,0:T(8,128)(2,1)S(1)} %get-tuple-element.389), channel_id=1, source_target_pairs={{0,4},{4,8},{8,12},{12,16},{16,20},{20,24},{24,28},{28,0},{1,5},{5... | collective-permute-start | bytes 196616 | tf_op jit(solution)/shard_map/while/body/eval_jaxpr/ppermute | solution.py:15
  56.8 2.2 %multiply_convert_fusion.9 = (bf16[128,512]{1,0:T(8,128)(2,1)S(1)}, bf16[128,512]{1,0:T(8,128)(2,1)S(1)}, bf16[128,512]{1,0:T(8,128)(2,1)S(1)}, bf16[128,512]{1,0:T(8,128)(2,1)S(1)}) fusion(f32[128]{0:T(128)S(1)} %get-tuple-element.360, f32[128]{0:T(128)S(1)} %get-tuple-element.361, f32[512]{0:T(512)S(1)} %bitcast.146, f32[512]{0:T(512)S(1)} %bitcast.145, ...), kind=kLoop, calls=%fused_computation.27.clone.1 | loop fusion | flops 1310720 | bytes 530432 | tf_op jit(solution)/shard_map/while/body/eval_jaxpr/convert_element_type | solution.py:39
  59.4 2.7 %collective-permute-done = bf16[2,128,128]{2,1,0:T(8,128)(2,1)S(1)} collective-permute-done((bf16[2,128,128]{2,1,0:T(8,128)(2,1)S(1)}, bf16[2,128,128]{2,1,0:T(8,128)(2,1)S(1)}, u32[]{:S(2)}, u32[]{:S(2)}) %collective-permute-start) | collective-permute-done | bytes 65568 | tf_op jit(solution)/shard_map/while/body/eval_jaxpr/ppermute | solution.py:15
  63.6 0.7 gather_fusion
  64.4 1.3 %collective-permute-start.3 = (f32[2,128,64]{2,1,0:T(8,128)S(1)}, f32[2,128,64]{2,1,0:T(8,128)S(1)}, u32[]{:S(2)}, u32[]{:S(2)}) collective-permute-start(f32[2,128,64]{2,1,0:T(8,128)S(1)} %select_bitcast_fusion.1), channel_id=1, source_target_pairs={{0,1},{1,2},{2,3},{3,4},{4,5},{5,6},{6,7},{7,8},{8,9},{9,10},{10,1... | collective-permute-start | bytes 196616 | tf_op jit(solution)/shard_map/ppermute | solution.py:26
  66.5 1.3 %collective-permute-start.4 = (f32[2,128,64]{2,1,0:T(8,128)S(1)}, f32[2,128,64]{2,1,0:T(8,128)S(1)}, u32[]{:S(2)}, u32[]{:S(2)}) collective-permute-start(f32[2,128,64]{2,1,0:T(8,128)S(1)} %select_bitcast_fusion), channel_id=1, source_target_pairs={{1,0},{2,1},{3,2},{4,3},{5,4},{6,5},{7,6},{8,7},{9,8},{10,9},{11,1... | collective-permute-start | bytes 196616 | tf_op jit(solution)/shard_map/ppermute | solution.py:28
  68.0 1.9 %collective-permute-done.2 = bf16[2,128,128]{2,1,0:T(8,128)(2,1)S(1)} collective-permute-done((bf16[2,128,128]{2,1,0:T(8,128)(2,1)S(1)}, bf16[2,128,128]{2,1,0:T(8,128)(2,1)S(1)}, u32[]{:S(2)}, u32[]{:S(2)}) %collective-permute-start.2) | collective-permute-done | bytes 65568 | tf_op jit(solution)/shard_map/ppermute | solution.py:15
  70.2 0.9 maximum_add_fusion.1
  71.1 0.7 copy-done.2
  71.8 0.7 copy-done.1
  72.8 0.7 gather_fusion.2
  73.6 0.7 gather_fusion.3
  74.5 0.8 gather_fusion.4
  75.4 0.7 gather_fusion.5
  76.2 0.7 gather_fusion.6
  77.1 0.7 gather_fusion.7
  78.0 17.4 %reduce-scatter.2.cloned.1.call-done = f32[2,128,128]{2,1,0:T(8,128)} async-done(((f32[2,128,512]{2,1,0:T(8,128)}), f32[2,128,128]{2,1,0:T(8,128)}) %reduce-scatter.2.cloned.1.call-update) | async-done | bytes 131088 | tf_op jit(solution)/shard_map/reduce_scatter | solution.py:95
  95.5 0.9 slice_subtract_fusion.4
  96.4 0.7 pad_maximum_fusion.2
  (83 shorter events, 7.5 us)
Async XLA Ops:
  6.5 88.9 %reduce-scatter.2.cloned.1.call-start = ((), (), s32[]{:S(2)}) async-start(), calls=%async_computation.1 | async-start | bytes 655360 | tf_op jit(solution)/shard_map/reduce_scatter | solution.py:95
  6.5 0.7 copy-start
  38.5 4.4 %collective-permute-start.1 = (bf16[2,128,128]{2,1,0:T(8,128)(2,1)S(1)}, bf16[2,128,128]{2,1,0:T(8,128)(2,1)S(1)}, u32[]{:S(2)}, u32[]{:S(2)}) collective-permute-start(bf16[2,128,128]{2,1,0:T(8,128)(2,1)S(1)} %get-tuple-element.390), channel_id=1, source_target_pairs={{0,28},{4,0},{8,4},{12,8},{16,12},{20,16},{24,20},{28,24},{1,29},{... | collective-permute-start | bytes 196616 | tf_op jit(solution)/shard_map/while/body/eval_jaxpr/ppermute | solution.py:15
  38.6 7.1 %collective-permute-start = (bf16[2,128,128]{2,1,0:T(8,128)(2,1)S(1)}, bf16[2,128,128]{2,1,0:T(8,128)(2,1)S(1)}, u32[]{:S(2)}, u32[]{:S(2)}) collective-permute-start(bf16[2,128,128]{2,1,0:T(8,128)(2,1)S(1)} %get-tuple-element.389), channel_id=1, source_target_pairs={{0,4},{4,8},{8,12},{12,16},{16,20},{20,24},{24,28},{28,0},{1,5},{5... | collective-permute-start | bytes 196616 | tf_op jit(solution)/shard_map/while/body/eval_jaxpr/ppermute | solution.py:15
  46.3 4.3 %collective-permute-start.1 = (bf16[2,128,128]{2,1,0:T(8,128)(2,1)S(1)}, bf16[2,128,128]{2,1,0:T(8,128)(2,1)S(1)}, u32[]{:S(2)}, u32[]{:S(2)}) collective-permute-start(bf16[2,128,128]{2,1,0:T(8,128)(2,1)S(1)} %get-tuple-element.390), channel_id=1, source_target_pairs={{0,28},{4,0},{8,4},{12,8},{16,12},{20,16},{24,20},{28,24},{1,29},{... | collective-permute-start | bytes 196616 | tf_op jit(solution)/shard_map/while/body/eval_jaxpr/ppermute | solution.py:15
  47.0 7.0 %collective-permute-start = (bf16[2,128,128]{2,1,0:T(8,128)(2,1)S(1)}, bf16[2,128,128]{2,1,0:T(8,128)(2,1)S(1)}, u32[]{:S(2)}, u32[]{:S(2)}) collective-permute-start(bf16[2,128,128]{2,1,0:T(8,128)(2,1)S(1)} %get-tuple-element.389), channel_id=1, source_target_pairs={{0,4},{4,8},{8,12},{12,16},{16,20},{20,24},{24,28},{28,0},{1,5},{5... | collective-permute-start | bytes 196616 | tf_op jit(solution)/shard_map/while/body/eval_jaxpr/ppermute | solution.py:15
  54.7 4.3 %collective-permute-start.1 = (bf16[2,128,128]{2,1,0:T(8,128)(2,1)S(1)}, bf16[2,128,128]{2,1,0:T(8,128)(2,1)S(1)}, u32[]{:S(2)}, u32[]{:S(2)}) collective-permute-start(bf16[2,128,128]{2,1,0:T(8,128)(2,1)S(1)} %get-tuple-element.390), channel_id=1, source_target_pairs={{0,28},{4,0},{8,4},{12,8},{16,12},{20,16},{24,20},{28,24},{1,29},{... | collective-permute-start | bytes 196616 | tf_op jit(solution)/shard_map/while/body/eval_jaxpr/ppermute | solution.py:15
  55.2 7.0 %collective-permute-start = (bf16[2,128,128]{2,1,0:T(8,128)(2,1)S(1)}, bf16[2,128,128]{2,1,0:T(8,128)(2,1)S(1)}, u32[]{:S(2)}, u32[]{:S(2)}) collective-permute-start(bf16[2,128,128]{2,1,0:T(8,128)(2,1)S(1)} %get-tuple-element.389), channel_id=1, source_target_pairs={{0,4},{4,8},{8,12},{12,16},{16,20},{20,24},{24,28},{28,0},{1,5},{5... | collective-permute-start | bytes 196616 | tf_op jit(solution)/shard_map/while/body/eval_jaxpr/ppermute | solution.py:15
  62.8 7.0 %collective-permute-start.2 = (bf16[2,128,128]{2,1,0:T(8,128)(2,1)S(1)}, bf16[2,128,128]{2,1,0:T(8,128)(2,1)S(1)}, u32[]{:S(2)}, u32[]{:S(2)}) collective-permute-start(bf16[2,128,128]{2,1,0:T(8,128)(2,1)S(1)} %get-tuple-element.186), channel_id=1, source_target_pairs={{0,4},{4,8},{8,12},{12,16},{16,20},{20,24},{24,28},{28,0},{1,5},{5... | collective-permute-start | bytes 196616 | tf_op jit(solution)/shard_map/ppermute | solution.py:15
  62.9 0.7 copy-start.3
  64.4 8.1 %collective-permute-start.3 = (f32[2,128,64]{2,1,0:T(8,128)S(1)}, f32[2,128,64]{2,1,0:T(8,128)S(1)}, u32[]{:S(2)}, u32[]{:S(2)}) collective-permute-start(f32[2,128,64]{2,1,0:T(8,128)S(1)} %select_bitcast_fusion.1), channel_id=1, source_target_pairs={{0,1},{1,2},{2,3},{3,4},{4,5},{5,6},{6,7},{7,8},{8,9},{9,10},{10,1... | collective-permute-start | bytes 196616 | tf_op jit(solution)/shard_map/ppermute | solution.py:26
  66.5 6.1 %collective-permute-start.4 = (f32[2,128,64]{2,1,0:T(8,128)S(1)}, f32[2,128,64]{2,1,0:T(8,128)S(1)}, u32[]{:S(2)}, u32[]{:S(2)}) collective-permute-start(f32[2,128,64]{2,1,0:T(8,128)S(1)} %select_bitcast_fusion), channel_id=1, source_target_pairs={{1,0},{2,1},{3,2},{4,3},{5,4},{6,5},{7,6},{8,7},{9,8},{10,9},{11,1... | collective-permute-start | bytes 196616 | tf_op jit(solution)/shard_map/ppermute | solution.py:28
  71.1 0.7 copy-start.2
  71.8 0.7 copy-start.1
  77.9 17.5 %copy-start.4 = (f32[128]{0:T(128)S(1)}, f32[128]{0:T(128)}, u32[]{:S(2)}) copy-start(f32[128]{0:T(128)} %param.18) | copy-start | bytes 1540
  77.9 17.5 %copy-start.5 = (f32[128]{0:T(128)S(1)}, f32[128]{0:T(128)}, u32[]{:S(2)}) copy-start(f32[128]{0:T(128)} %param.17) | copy-start | bytes 1540
Sparse Core Ops, SparseCore 0:
  71.2 24.1 reduce-scatter.1
where the time goes:
time: 104 us
  blocking collectives  27.4 us (26%)
  waiting for transfers between devices  27.3 us (26%)
  other arithmetic  14 us (13%)
  between operations  13.7 us (13%)
  local copies, waits for them, and re-layouts  9.91 us (10%)
  starting transfers between devices  8.88 us (9%)
  matrix products  2.5 us (2%)
    all_gather x1, blocking collectives, local(): source_place = lax.all_gather(positions, 'blk', axis=1, tiled=True)  22.3 us
    reduce_scatter x1, waiting for transfers between devices, local(): fresnel = lax.psum_scatter(total, 'grp', scatter_dimension=2, tiled=True)  17.4 us
    ppermute x7, waiting for transfers between devices, from_behind(): lax.ppermute(array, axis, [(i, (i + by) % size) for i in range(size)])  9.9 us
    convert_element_type x4, other arithmetic, kernel_table(): cosine = (scaled * jnp.cos(phase)).astype(jnp.bfloat16)  8.92 us
    ppermute x7, starting transfers between devices, from_behind(): lax.ppermute(array, axis, [(i, (i + by) % size) for i in range(size)])  6.29 us
    gather x12, local copies, waits for them, and re-layouts, local(): picked = jnp.take(local_buffer, neighbours[neighbour_slot], axis=2)  5.06 us
    all_gather x1, blocking collectives, local(): target_place = lax.all_gather(positions, 'grp', axis=1, tiled=True)  5.05 us
    unnamed x13, local copies, waits for them, and re-layouts  2.59 us
  transfers between devices with their start and end apart: 10, of which 6 were waited for; matrix products, arithmetic and copies ran while one was open for 16% of the time, Pallas kernels for 0%

commit v1 on v0

v1 whole, which is shorter than its diff:
```python
import math

import jax
import jax.numpy as jnp
from jax import lax
from jax.sharding import PartitionSpec as P

section_weight = 0.25
phase_rate = 60.0
alpha_factor = 2.0
ALL = ("blk", "grp")


def bf16_pieces(value):
    high = lax.reduce_precision(value, exponent_bits=8, mantissa_bits=7)
    rest = value - high
    middle = lax.reduce_precision(rest, exponent_bits=8, mantissa_bits=7)
    low = rest - middle
    return [p.astype(jnp.bfloat16) for p in (high, middle, low)]


def from_pieces(high, middle, low):
    f32 = jnp.float32
    return high.astype(f32) + (middle.astype(f32) + low.astype(f32))


def kernel_table(source_place, target_place, scaled):
    horizontal = target_place[0][None, :] - source_place[0][:, None]
    vertical = target_place[1][None, :] - source_place[1][:, None]
    phase = phase_rate * (horizontal * horizontal + vertical * vertical)
    cosine = (scaled * jnp.cos(phase)).astype(jnp.bfloat16)
    sine_part = (scaled * jnp.sin(phase)).astype(jnp.bfloat16)
    return jnp.concatenate([cosine, sine_part], axis=1)


def block_product(fields, source_place, target_place, scaled):
    kernel = kernel_table(source_place, target_place, scaled)
    flat = fields.reshape(2 * fields.shape[1], fields.shape[2])
    return jnp.dot(flat, kernel, preferred_element_type=jnp.float32)


def local(state, prev_slope, positions, pump, detuning, kappa, neighbours, send_list):
    members = state.shape[1]
    rows_here = state.shape[2]
    devices = lax.axis_size(ALL)
    scaled = 1.0 / math.sqrt(rows_here * devices)
    section_field = state + section_weight * prev_slope
    section_half = section_field.astype(jnp.bfloat16)

    to_prev = jnp.take(section_field, send_list[1], axis=2)
    to_next = jnp.take(section_field, send_list[0], axis=2)
    from_prev = lax.ppermute(to_next, ALL, [(i, i + 1) for i in range(devices - 1)])
    from_next = lax.ppermute(to_prev, ALL, [(i + 1, i) for i in range(devices - 1)])

    pieces = jnp.stack(bf16_pieces(positions), axis=1)
    payload = jnp.concatenate([section_half, pieces], axis=1)

    product = block_product(section_half, positions, positions, scaled)
    gathered = payload
    mask = devices // 2
    while mask >= 1:
        received = lax.ppermute(gathered, ALL, [(i, i ^ mask) for i in range(devices)])
        place = from_pieces(
            received[:, members], received[:, members + 1], received[:, members + 2]
        )
        product = product + block_product(received[:, :members], place, positions, scaled)
        gathered = jnp.concatenate([gathered, received], axis=2)
        mask //= 2
    real_part = product[:members, :rows_here] - product[members:, rows_here:]
    imag_part = product[:members, rows_here:] + product[members:, :rows_here]

    local_buffer = jnp.concatenate([section_field, from_prev, from_next], axis=2)
    coupled = jnp.zeros((2, members, rows_here), jnp.float32)
    for neighbour_slot in range(kappa.shape[0]):
        picked = jnp.take(local_buffer, neighbours[neighbour_slot], axis=2)
        coupled = coupled + kappa[neighbour_slot] * picked
    real_field = section_field[0]
    imag_field = section_field[1]
    modulus = real_field * real_field + imag_field * imag_field
    linear_real = pump - modulus
    linear_imag = detuning - alpha_factor * modulus
    local_real = linear_real * real_field - linear_imag * imag_field
    local_imag = linear_real * imag_field + linear_imag * real_field
    slope_real = local_real + real_part - coupled[1]
    slope_imag = local_imag + imag_part + coupled[0]
    return jnp.stack([slope_real, slope_imag])


def solution(mesh):
    placed = (
        P(None, None, ALL),
        P(None, None, ALL),
        P(None, ALL),
        P(ALL),
        P(ALL),
        P(None, ALL),
        P(None, ALL),
        P(None, ALL),
    )
    return jax.shard_map(
        local, mesh=mesh, in_specs=placed, out_specs=P(None, None, ALL), check_vma=False
    )
```

time: 104 us -> 63.4 us (0.61)
  blocking collectives: 27.4 us -> 0 us
  between operations: 13.7 us -> 0.6 us
  starting transfers between devices: 8.88 us -> 13.9 us
  waiting for transfers between devices: 27.3 us -> 23.5 us
    all_gather x2 -> x0, blocking collectives: 27.4 us -> none  [the longest x1 22.3 us: local(): source_place = lax.all_gather(positions, 'blk', axis=1, tiled=True)]
    reduce_scatter x1 -> x0, waiting for transfers between devices: 17.4 us -> none  [local(): fresnel = lax.psum_scatter(total, 'grp', scatter_dimension=2, tiled=True)]
    ppermute x9 -> x7, waiting for transfers between devices: 9.9 us -> 23.5 us  [the longest x5 20.2 us: local(): lax.ppermute(gathered, ALL, [(i, i ^ mask) for i in range(devices)])]
    ppermute x9 -> x7, starting transfers between devices: 8.88 us -> 13.9 us  [the longest x5 11.1 us: local(): lax.ppermute(gathered, ALL, [(i, i ^ mask) for i in range(devices)])]
    add x4 -> x5, other arithmetic: 1.69 us -> 0.05 us  [from_pieces(): return high.astype(f32) + (middle.astype(f32) + low.astype(f32))]
    slice x0 -> x7, local copies, waits for them, and re-layouts: none -> 1.53 us  [local(): received[:, :members]]
    unnamed x13 -> x20, local copies, waits for them, and re-layouts: 2.59 us -> 1.07 us
    dot_general x8 -> x6, matrix products: 2.5 us -> 1.5 us  [block_product(): return jnp.dot(flat, kernel, preferred_element_type=jnp.float32)]
  transfers between devices with their start and end apart: 10 -> 7, of which waited for: 6 -> 4; matrix products, arithmetic and copies ran while one was open for 16% -> 24% of each run, Pallas kernels for 0% -> 0%
where the time goes in v1:
time: 63.4 us; the launch traced here: 63.1 us
  waiting for transfers between devices  23.5 us (37%)
  starting transfers between devices  13.9 us (22%)
  other arithmetic  13.2 us (21%)
  local copies, waits for them, and re-layouts  10.5 us (17%)
  matrix products  1.5 us (2%)
    ppermute x5, waiting for transfers between devices, local(): lax.ppermute(gathered, ALL, [(i, i ^ mask) for i in range(devices)])  20.2 us
    ppermute x5, starting transfers between devices, local(): lax.ppermute(gathered, ALL, [(i, i ^ mask) for i in range(devices)])  11.1 us
    convert_element_type x5, other arithmetic, kernel_table(): cosine = (scaled * jnp.cos(phase)).astype(jnp.bfloat16)  9.57 us
    gather x12, local copies, waits for them, and re-layouts, local(): picked = jnp.take(local_buffer, neighbours[neighbour_slot], axis=2)  5.06 us
    ppermute x1, waiting for transfers between devices, local(): lax.ppermute(to_prev, ALL, [(i + 1, i) for i in range(devices - 1)])  3.3 us
    slice x7, local copies, waits for them, and re-layouts, local(): received[:, :members]  1.53 us
    dot_general x6, matrix products, block_product(): return jnp.dot(flat, kernel, preferred_element_type=jnp.float32)  1.5 us
    ppermute x1, starting transfers between devices, local(): lax.ppermute(to_next, ALL, [(i, i + 1) for i in range(devices - 1)])  1.47 us
  transfers between devices with their start and end apart: 7, of which 4 were waited for; matrix products, arithmetic and copies ran while one was open for 24% of the time, Pallas kernels for 0%

profile of v1, /device:TPU:0, one launch (start us, length us, event | category | flops | bytes accessed | tf_op | source)
XLA Modules:
  0.0 63.1 jit_solution(14201451546621816148)
XLA Ops:
  0.0 0.7 %fusion.43 = (bf16[2,1,128]{2,0,1:T(2,128)(2,1)S(1)}, bf16[2,1,128]{2,0,1:T(2,128)(2,1)S(1)}, bf16[2,1,128]{2,0,1:T(2,128)(2,1)S(1)}) fusion(f32[2,128]{1,0:T(2,128)} %param.14), kind=kLoop, calls=%fused_computation.138 | loop fusion | flops 1792 | bytes 2560 | tf_op jit(solution)/shard_map/stack | solution.py:55
  0.7 1.0 %fusion.52 = (bf16[2,128,128]{2,1,0:T(8,128)(2,1)S(1)}, f32[2,128,128]{2,1,0:T(8,128)S(1)}) fusion(f32[2,128,128]{2,1,0:T(8,128)} %param.12, f32[2,128,128]{2,1,0:T(8,128)} %param.13), kind=kLoop, calls=%fused_computation.157 | loop fusion | flops 98304 | bytes 458752 | tf_op jit(solution)/shard_map/convert_element_type | solution.py:48
  1.8 4.1 %collective-permute-start = (bf16[2,131,128]{2,1,0:T(8,128)(2,1)S(1)}, bf16[2,131,128]{2,1,0:T(8,128)(2,1)S(1)}, u32[]{:S(2)}, u32[]{:S(2)}) collective-permute-start(bf16[2,131,128]{2,1,0:T(8,128)(2,1)S(1)} %pad_maximum_fusion.5), channel_id=1, source_target_pairs={{0,16},{1,17},{2,18},{3,19},{4,20},{5,21},{6,22},{7,23},{8,24},{9,... | collective-permute-start | bytes 201224 | tf_op jit(solution)/shard_map/ppermute | solution.py:62
  6.0 0.8 %compare_and_fusion.7 = (pred[64]{0:T(512)(128)(4,1)S(1)}, s32[64]{0:T(128)S(1)}, pred[64]{0:T(512)(128)(4,1)S(1)}, s32[64]{0:T(128)S(1)}) fusion(s32[2,64]{1,0:T(2,128)} %param.19), kind=kLoop, calls=%fused_computation.127 | loop fusion | flops 768 | bytes 1152 | tf_op jit(solution)/shard_map/jit(_take)/and | solution.py:51
  6.8 0.7 %gather_fusion = f32[64,2,128]{2,1,0:T(2,128)S(1)} fusion(f32[2,128,128]{1,0,2:T(2,128)S(1)} %copy.100, s32[1024]{0:T(1024)S(1)} %pad_clamp_fusion.7), kind=kCustom, calls=%fused_computation.clone | custom fusion | bytes 131328 | tf_op jit(solution)/shard_map/jit(_take)/gather | solution.py:51
  7.6 1.5 %collective-permute-start.5 = (f32[2,128,64]{2,1,0:T(8,128)S(1)}, f32[2,128,64]{2,1,0:T(8,128)S(1)}, u32[]{:S(2)}, u32[]{:S(2)}) collective-permute-start(f32[2,128,64]{2,1,0:T(8,128)S(1)} %select_bitcast_fusion.1), channel_id=1, source_target_pairs={{0,1},{1,2},{2,3},{3,4},{4,5},{5,6},{6,7},{7,8},{8,9},{9,10},{10,1... | collective-permute-start | bytes 196616 | tf_op jit(solution)/shard_map/ppermute | solution.py:52
  9.0 0.7 %gather_fusion.1 = f32[64,2,128]{2,1,0:T(2,128)S(1)} fusion(f32[2,128,128]{1,0,2:T(2,128)S(1)} %copy.100, s32[1024]{0:T(1024)S(1)} %pad_clamp_fusion.6), kind=kCustom, calls=%fused_computation.2.clone | custom fusion | bytes 131328 | tf_op jit(solution)/shard_map/jit(_take)/gather | solution.py:50
  9.8 1.3 %collective-permute-start.6 = (f32[2,128,64]{2,1,0:T(8,128)S(1)}, f32[2,128,64]{2,1,0:T(8,128)S(1)}, u32[]{:S(2)}, u32[]{:S(2)}) collective-permute-start(f32[2,128,64]{2,1,0:T(8,128)S(1)} %select_bitcast_fusion), channel_id=1, source_target_pairs={{1,0},{2,1},{3,2},{4,3},{5,4},{6,5},{7,6},{8,7},{9,8},{10,9},{11,1... | collective-permute-start | bytes 196616 | tf_op jit(solution)/shard_map/ppermute | solution.py:53
  11.3 3.3 %collective-permute-done.6 = f32[2,128,64]{2,1,0:T(8,128)S(1)} collective-permute-done((f32[2,128,64]{2,1,0:T(8,128)S(1)}, f32[2,128,64]{2,1,0:T(8,128)S(1)}, u32[]{:S(2)}, u32[]{:S(2)}) %collective-permute-start.6) | collective-permute-done | bytes 65568 | tf_op jit(solution)/shard_map/ppermute | solution.py:53
  14.9 0.7 %gather_fusion.2 = f32[128,2,128]{2,1,0:T(2,128)S(1)} fusion(f32[2,128,256]{1,0,2:T(2,128)S(1)} %copy.104, s32[1024]{0:T(1024)S(1)} %get-tuple-element.77), kind=kCustom, calls=%fused_computation.1.clone | custom fusion | bytes 262656 | tf_op jit(solution)/shard_map/jit(_take)/gather | solution.py:75
  15.7 0.7 %gather_fusion.3 = f32[128,2,128]{2,1,0:T(2,128)S(1)} fusion(f32[2,128,256]{1,0,2:T(2,128)S(1)} %copy.104, s32[1024]{0:T(1024)S(1)} %get-tuple-element.76), kind=kCustom, calls=%fused_computation.3.clone | custom fusion | bytes 262656 | tf_op jit(solution)/shard_map/jit(_take)/gather | solution.py:75
  16.6 0.7 %gather_fusion.4 = f32[128,2,128]{2,1,0:T(2,128)S(1)} fusion(f32[2,128,256]{1,0,2:T(2,128)S(1)} %copy.104, s32[1024]{0:T(1024)S(1)} %get-tuple-element.75), kind=kCustom, calls=%fused_computation.4.clone | custom fusion | bytes 262656 | tf_op jit(solution)/shard_map/jit(_take)/gather | solution.py:75
  17.4 0.8 %gather_fusion.5 = f32[128,2,128]{2,1,0:T(2,128)S(1)} fusion(f32[2,128,256]{1,0,2:T(2,128)S(1)} %copy.104, s32[1024]{0:T(1024)S(1)} %get-tuple-element.74), kind=kCustom, calls=%fused_computation.5.clone | custom fusion | bytes 262656 | tf_op jit(solution)/shard_map/jit(_take)/gather | solution.py:75
  18.3 0.7 %gather_fusion.6 = f32[128,2,128]{2,1,0:T(2,128)S(1)} fusion(f32[2,128,256]{1,0,2:T(2,128)S(1)} %copy.104, s32[1024]{0:T(1024)S(1)} %get-tuple-element.73), kind=kCustom, calls=%fused_computation.6.clone | custom fusion | bytes 262656 | tf_op jit(solution)/shard_map/jit(_take)/gather | solution.py:75
  19.2 0.8 %gather_fusion.7 = f32[128,2,128]{2,1,0:T(2,128)S(1)} fusion(f32[2,128,256]{1,0,2:T(2,128)S(1)} %copy.104, s32[1024]{0:T(1024)S(1)} %get-tuple-element.72), kind=kCustom, calls=%fused_computation.7.clone | custom fusion | bytes 262656 | tf_op jit(solution)/shard_map/jit(_take)/gather | solution.py:75
  20.2 5.2 %collective-permute-start.1 = (bf16[2,131,256]{2,1,0:T(8,128)(2,1)S(1)}, bf16[2,131,256]{2,1,0:T(8,128)(2,1)S(1)}, u32[]{:S(2)}, u32[]{:S(2)}) collective-permute-start(bf16[2,131,256]{2,1,0:T(8,128)(2,1)S(1)} %pad_maximum_fusion.3), channel_id=1, source_target_pairs={{0,8},{1,9},{2,10},{3,11},{4,12},{5,13},{6,14},{7,15},{8,0},{9,1},... | collective-permute-start | bytes 402440 | tf_op jit(solution)/shard_map/ppermute | solution.py:62
  25.4 0.6 multiply_convert_fusion.9
  26.5 2.8 %collective-permute-done.1 = bf16[2,131,256]{2,1,0:T(8,128)(2,1)S(1)} collective-permute-done((bf16[2,131,256]{2,1,0:T(8,128)(2,1)S(1)}, bf16[2,131,256]{2,1,0:T(8,128)(2,1)S(1)}, u32[]{:S(2)}, u32[]{:S(2)}) %collective-permute-start.1) | collective-permute-done | bytes 134176 | tf_op jit(solution)/shard_map/ppermute | solution.py:62
  29.4 1.6 %collective-permute-start.2 = (bf16[2,131,512]{2,1,0:T(8,128)(2,1)S(1)}, bf16[2,131,512]{2,1,0:T(8,128)(2,1)S(1)}, u32[]{:S(2)}, u32[]{:S(2)}) collective-permute-start(bf16[2,131,512]{2,1,0:T(8,128)(2,1)S(1)} %pad_maximum_fusion.1), channel_id=1, source_target_pairs={{0,4},{1,5},{2,6},{3,7},{4,0},{5,1},{6,2},{7,3},{8,12},{9,13},{10,... | collective-permute-start | bytes 804872 | tf_op jit(solution)/shard_map/ppermute | solution.py:62
  31.0 0.6 multiply_convert_fusion.7
  31.7 6.0 %collective-permute-done.2 = bf16[2,131,512]{2,1,0:T(8,128)(2,1)S(1)} collective-permute-done((bf16[2,131,512]{2,1,0:T(8,128)(2,1)S(1)}, bf16[2,131,512]{2,1,0:T(8,128)(2,1)S(1)}, u32[]{:S(2)}, u32[]{:S(2)}) %collective-permute-start.2) | collective-permute-done | bytes 268320 | tf_op jit(solution)/shard_map/ppermute | solution.py:62
  37.8 0.6 copy.93
  38.5 1.3 %multiply_convert_fusion.5 = (bf16[512,128]{1,0:T(8,128)(2,1)S(1)}, bf16[512,128]{1,0:T(8,128)(2,1)S(1)}) fusion(f32[512]{0:T(512)S(1)} %bitcast.145, f32[128]{0:T(128)S(1)} %get-tuple-element.66, f32[512]{0:T(512)S(1)} %bitcast.144, f32[128]{0:T(128)S(1)} %get-tuple-element.65), kind=kLoop, calls=%fused_computation.36 | loop fusion | flops 655360 | bytes 267264 | tf_op jit(solution)/shard_map/convert_element_type | solution.py:31
  40.1 11.4 %collective-permute-done.3 = bf16[2,131,1024]{2,0,1:T(2,128)(2,1)S(1)} collective-permute-done((bf16[2,131,1024]{2,0,1:T(2,128)(2,1)S(1)}, bf16[2,131,1024]{2,0,1:T(2,128)(2,1)S(1)}, u32[]{:S(2)}, u32[]{:S(2)}) %collective-permute-start.3) | collective-permute-done | bytes 536608 | tf_op jit(solution)/shard_map/ppermute | solution.py:62
  51.5 0.4 constant_dynamic-update-slice_fusion
  52.2 0.4 slice.274
  52.7 2.6 %multiply_convert_fusion.3 = (bf16[1024,128]{1,0:T(8,128)(2,1)S(1)}, bf16[1024,128]{1,0:T(8,128)(2,1)S(1)}) fusion(f32[1024]{0:T(1024)S(1)} %bitcast.143, f32[128]{0:T(128)S(1)} %get-tuple-element.66, f32[1024]{0:T(1024)S(1)} %bitcast.142, f32[128]{0:T(128)S(1)} %get-tuple-element.65), kind=kLoop, calls=%fused_computation.26 | loop fusion | flops 1310720 | bytes 533504 | tf_op jit(solution)/shard_map/convert_element_type | solution.py:31
  55.7 0.7 %slice.280 = bf16[2,128,2048]{2,0,1:T(2,128)(2,1)S(1)} slice(bf16[2,131,2048]{2,0,1:T(2,128)(2,1)S(1)} %collective-permute-done.4), slice={[0:2], [0:128], [0:2048]} | slice | bytes 2097152 | tf_op jit(solution)/shard_map/slice | solution.py:66
  56.7 4.5 %multiply_convert_fusion.1 = (bf16[2048,128]{1,0:T(8,128)(2,1)S(1)}, bf16[2048,128]{1,0:T(8,128)(2,1)S(1)}) fusion(f32[2048]{0:T(1024)S(1)} %bitcast.141, f32[128]{0:T(128)S(1)} %get-tuple-element.66, f32[2048]{0:T(1024)S(1)} %bitcast.140, f32[128]{0:T(128)S(1)} %get-tuple-element.65), kind=kLoop, calls=%fused_computation.18 | loop fusion | flops 2621440 | bytes 1065984 | tf_op jit(solution)/shard_map/convert_element_type | solution.py:31
  61.3 0.4 fusion.3
  61.7 0.4 slice-done.1
  62.5 0.7 %pad_maximum_fusion.4 = f32[2,128,128]{2,1,0:T(8,128)} fusion(f32[1,128,128]{2,1,0:T(8,128)S(1)} %get-tuple-element.26, f32[1,128,128]{2,1,0:T(8,128)S(1)} %get-tuple-element.25), kind=kLoop, calls=%fused_computation.43 | loop fusion | flops 32768 | bytes 262144 | tf_op jit(solution)/shard_map/stack | solution.py:86
  (74 shorter events, 3.9 us)
Async XLA Ops:
  0.7 10.4 %copy-start.2 = (f32[2,128]{1,0:T(2,128)S(1)}, f32[2,128]{1,0:T(2,128)}, u32[]{:S(2)}) copy-start(f32[2,128]{1,0:T(2,128)} %param.14) | copy-start | bytes 3076
  1.7 9.5 %copy-start.4 = (s32[6,128]{1,0:T(8,128)S(1)}, s32[6,128]{1,0:T(8,128)}, u32[]{:S(2)}) copy-start(s32[6,128]{1,0:T(8,128)} %param.18) | copy-start | bytes 9220
  1.7 9.5 %copy-start.3 = (f32[6,128]{1,0:T(8,128)S(1)}, f32[6,128]{1,0:T(8,128)}, u32[]{:S(2)}) copy-start(f32[6,128]{1,0:T(8,128)} %param.17) | copy-start | bytes 9220
  1.8 18.4 %collective-permute-start = (bf16[2,131,128]{2,1,0:T(8,128)(2,1)S(1)}, bf16[2,131,128]{2,1,0:T(8,128)(2,1)S(1)}, u32[]{:S(2)}, u32[]{:S(2)}) collective-permute-start(bf16[2,131,128]{2,1,0:T(8,128)(2,1)S(1)} %pad_maximum_fusion.5), channel_id=1, source_target_pairs={{0,16},{1,17},{2,18},{3,19},{4,20},{5,21},{6,22},{7,23},{8,24},{9,... | collective-permute-start | bytes 201224 | tf_op jit(solution)/shard_map/ppermute | solution.py:62
  7.6 3.8 %collective-permute-start.5 = (f32[2,128,64]{2,1,0:T(8,128)S(1)}, f32[2,128,64]{2,1,0:T(8,128)S(1)}, u32[]{:S(2)}, u32[]{:S(2)}) collective-permute-start(f32[2,128,64]{2,1,0:T(8,128)S(1)} %select_bitcast_fusion.1), channel_id=1, source_target_pairs={{0,1},{1,2},{2,3},{3,4},{4,5},{5,6},{6,7},{7,8},{8,9},{9,10},{10,1... | collective-permute-start | bytes 196616 | tf_op jit(solution)/shard_map/ppermute | solution.py:52
  9.8 4.8 %collective-permute-start.6 = (f32[2,128,64]{2,1,0:T(8,128)S(1)}, f32[2,128,64]{2,1,0:T(8,128)S(1)}, u32[]{:S(2)}, u32[]{:S(2)}) collective-permute-start(f32[2,128,64]{2,1,0:T(8,128)S(1)} %select_bitcast_fusion), channel_id=1, source_target_pairs={{1,0},{2,1},{3,2},{4,3},{5,4},{6,5},{7,6},{8,7},{9,8},{10,9},{11,1... | collective-permute-start | bytes 196616 | tf_op jit(solution)/shard_map/ppermute | solution.py:53
  20.2 9.2 %collective-permute-start.1 = (bf16[2,131,256]{2,1,0:T(8,128)(2,1)S(1)}, bf16[2,131,256]{2,1,0:T(8,128)(2,1)S(1)}, u32[]{:S(2)}, u32[]{:S(2)}) collective-permute-start(bf16[2,131,256]{2,1,0:T(8,128)(2,1)S(1)} %pad_maximum_fusion.3), channel_id=1, source_target_pairs={{0,8},{1,9},{2,10},{3,11},{4,12},{5,13},{6,14},{7,15},{8,0},{9,1},... | collective-permute-start | bytes 402440 | tf_op jit(solution)/shard_map/ppermute | solution.py:62
  29.3 8.5 %copy-start.1 = (bf16[2,131,256]{2,1,0:T(8,128)(2,1)}, bf16[2,131,256]{2,1,0:T(8,128)(2,1)S(1)}, u32[]{:S(2)}) copy-start(bf16[2,131,256]{2,1,0:T(8,128)(2,1)S(1)} %collective-permute-done.1) | copy-start | bytes 402436
  29.4 8.4 %collective-permute-start.2 = (bf16[2,131,512]{2,1,0:T(8,128)(2,1)S(1)}, bf16[2,131,512]{2,1,0:T(8,128)(2,1)S(1)}, u32[]{:S(2)}, u32[]{:S(2)}) collective-permute-start(bf16[2,131,512]{2,1,0:T(8,128)(2,1)S(1)} %pad_maximum_fusion.1), channel_id=1, source_target_pairs={{0,4},{1,5},{2,6},{3,7},{4,0},{5,1},{6,2},{7,3},{8,12},{9,13},{10,... | collective-permute-start | bytes 804872 | tf_op jit(solution)/shard_map/ppermute | solution.py:62
  37.8 2.1 %copy-start = (bf16[2,131,512]{2,1,0:T(8,128)(2,1)}, bf16[2,131,512]{2,1,0:T(8,128)(2,1)S(1)}, u32[]{:S(2)}) copy-start(bf16[2,131,512]{2,1,0:T(8,128)(2,1)S(1)} %collective-permute-done.2) | copy-start | bytes 804868
  38.4 13.0 %collective-permute-start.3 = (bf16[2,131,1024]{2,0,1:T(2,128)(2,1)S(1)}, bf16[2,131,1024]{2,0,1:T(2,128)(2,1)S(1)}, u32[]{:S(2)}, u32[]{:S(2)}) collective-permute-start(bf16[2,131,1024]{2,0,1:T(2,128)(2,1)S(1)} %copy.93), channel_id=1, source_target_pairs={{0,2},{1,3},{2,0},{3,1},{4,6},{5,7},{6,4},{7,5},{8,10},{9,11},{10,... | collective-permute-start | bytes 1609736 | tf_op jit(solution)/shard_map/ppermute | solution.py:62
  40.1 11.9 %slice-start = ((bf16[2,131,512]{2,1,0:T(8,128)(2,1)}), bf16[2,128,512]{2,1,0:T(8,128)(2,1)S(1)}, s32[]{:S(2)}) async-start(bf16[2,131,512]{2,1,0:T(8,128)(2,1)} %copy-done), calls=%async_computation | async-start | bytes 524288 | tf_op jit(solution)/shard_map/slice | solution.py:66
  51.9 3.7 %collective-permute-start.4 = (bf16[2,131,2048]{2,0,1:T(2,128)(2,1)S(1)}, bf16[2,131,2048]{2,0,1:T(2,128)(2,1)S(1)}, u32[]{:S(2)}, u32[]{:S(2)}) collective-permute-start(bf16[2,131,2048]{2,0,1:T(2,128)(2,1)S(1)} %constant_dynamic-update-slice_fusion), channel_id=1, source_target_pairs={{0,1},{1,0},{2,3},{3,2},{4,5},{5,4},{6,7},{7,6},{8,9},{9,8},{10,11... | collective-permute-start | bytes 3219464 | tf_op jit(solution)/shard_map/ppermute | solution.py:62
  61.3 0.9 %slice-start.1 = ((bf16[2,131,256]{2,1,0:T(8,128)(2,1)}), bf16[2,128,256]{2,1,0:T(8,128)(2,1)S(1)}, s32[]{:S(2)}) async-start(bf16[2,131,256]{2,1,0:T(8,128)(2,1)} %copy-done.1), calls=%async_computation.1 | async-start | bytes 262144 | tf_op jit(solution)/shard_map/slice | solution.py:66
  61.7 0.7 %copy-start.5 = (f32[128]{0:T(128)S(1)}, f32[128]{0:T(128)}, u32[]{:S(2)}) copy-start(f32[128]{0:T(128)} %param.16) | copy-start | bytes 1540
  61.7 0.7 %copy-start.6 = (f32[128]{0:T(128)S(1)}, f32[128]{0:T(128)}, u32[]{:S(2)}) copy-start(f32[128]{0:T(128)} %param.15) | copy-start | bytes 1540

commit v2 on v1

--- a/solution.py
+++ b/solution.py
@@ -39,35 +39,72 @@
     return jnp.dot(flat, kernel, preferred_element_type=jnp.float32)
 
 
+def exchange(value, axis, mask):
+    count = lax.axis_size(axis)
+    return lax.ppermute(value, axis, [(i, i ^ mask) for i in range(count)])
+
+
 def local(state, prev_slope, positions, pump, detuning, kappa, neighbours, send_list):
     members = state.shape[1]
     rows_here = state.shape[2]
     devices = lax.axis_size(ALL)
+    blocks = lax.axis_size("blk")
+    group = lax.axis_size("grp")
     scaled = 1.0 / math.sqrt(rows_here * devices)
     section_field = state + section_weight * prev_slope
     section_half = section_field.astype(jnp.bfloat16)
+    where_in_group = lax.axis_index("grp")
 
     to_prev = jnp.take(section_field, send_list[1], axis=2)
     to_next = jnp.take(section_field, send_list[0], axis=2)
     from_prev = lax.ppermute(to_next, ALL, [(i, i + 1) for i in range(devices - 1)])
     from_next = lax.ppermute(to_prev, ALL, [(i + 1, i) for i in range(devices - 1)])
 
+    targets = positions
+    mask = 1
+    while mask < group:
+        other = exchange(targets, "grp", mask)
+        upper = (where_in_group & mask) != 0
+        targets = jnp.where(
+            upper,
+            jnp.concatenate([other, targets], axis=1),
+            jnp.concatenate([targets, other], axis=1),
+        )
+        mask *= 2
+    width = targets.shape[1]
+
     pieces = jnp.stack(bf16_pieces(positions), axis=1)
     payload = jnp.concatenate([section_half, pieces], axis=1)
-
-    product = block_product(section_half, positions, positions, scaled)
+    product = block_product(section_half, positions, targets, scaled)
     gathered = payload
-    mask = devices // 2
+    mask = blocks // 2
     while mask >= 1:
-        received = lax.ppermute(gathered, ALL, [(i, i ^ mask) for i in range(devices)])
+        received = exchange(gathered, "blk", mask)
         place = from_pieces(
             received[:, members], received[:, members + 1], received[:, members + 2]
         )
-        product = product + block_product(received[:, :members], place, positions, scaled)
+        product = product + block_product(received[:, :members], place, targets, scaled)
         gathered = jnp.concatenate([gathered, received], axis=2)
         mask //= 2
-    real_part = product[:members, :rows_here] - product[members:, rows_here:]
-    imag_part = product[:members, rows_here:] + product[members:, :rows_here]
+    partial = jnp.stack(
+        [
+            product[:members, :width] - product[members:, width:],
+            product[:members, width:] + product[members:, :width],
+        ]
+    )
+
+    mask = group // 2
+    while mask >= 1:
+        half = partial.shape[2] // 2
+        lower = partial[:, :, :half]
+        higher = partial[:, :, half:]
+        upper = (where_in_group & mask) != 0
+        keep = jnp.where(upper, higher, lower)
+        give = jnp.where(upper, lower, higher)
+        partial = keep + exchange(give, "grp", mask)
+        mask //= 2
+    real_part = partial[0]
+    imag_part = partial[1]
 
     local_buffer = jnp.concatenate([section_field, from_prev, from_next], axis=2)
     coupled = jnp.zeros((2, members, rows_here), jnp.float32)

time: 63.4 us -> 46.5 us (0.73)
  the two profiles are of different devices: /device:TPU:0 before, /device:TPU:31 now
where the time goes in v2:
time: 46.5 us; the launch traced here: 46.3 us
  waiting for transfers between devices  15 us (32%)
  other arithmetic  12.1 us (26%)
  starting transfers between devices  10 us (22%)
  local copies, waits for them, and re-layouts  7.39 us (16%)
  matrix products  1.29 us (3%)
  between operations  0.51 us (1%)
    ppermute x7, waiting for transfers between devices, exchange(): return lax.ppermute(value, axis, [(i, i ^ mask) for i in range(count)])  15 us
    convert_element_type x3, other arithmetic, kernel_table(): cosine = (scaled * jnp.cos(phase)).astype(jnp.bfloat16)  9.04 us
    ppermute x7, starting transfers between devices, exchange(): return lax.ppermute(value, axis, [(i, i ^ mask) for i in range(count)])  6.15 us
    gather x12, local copies, waits for them, and re-layouts, local(): picked = jnp.take(local_buffer, neighbours[neighbour_slot], axis=2)  5.06 us
    ppermute x1, starting transfers between devices, local(): lax.ppermute(to_prev, ALL, [(i + 1, i) for i in range(devices - 1)])  2.59 us
    ppermute x1, starting transfers between devices, local(): lax.ppermute(to_next, ALL, [(i, i + 1) for i in range(devices - 1)])  1.29 us
    dot_general x4, matrix products, block_product(): return jnp.dot(flat, kernel, preferred_element_type=jnp.float32)  1.29 us
    convert_element_type x1, other arithmetic, local(): section_half = section_field.astype(jnp.bfloat16)  1 us
  transfers between devices with their start and end apart: 9, of which 6 were waited for; matrix products, arithmetic and copies ran while one was open for 36% of the time, Pallas kernels for 0%

profile of v2, /device:TPU:31, one launch (start us, length us, event | category | flops | bytes accessed | tf_op | source)
XLA Modules:
  0.0 46.3 jit_solution(10202659699600842054)
XLA Ops:
  0.0 1.0 %fusion.37 = (bf16[2,128,128]{2,1,0:T(8,128)(2,1)S(1)}, f32[2,128,128]{2,1,0:T(8,128)S(1)}) fusion(f32[2,128,128]{2,1,0:T(8,128)} %param.12, f32[2,128,128]{2,1,0:T(8,128)} %param.13), kind=kLoop, calls=%fused_computation.137 | loop fusion | flops 98304 | bytes 458752 | tf_op jit(solution)/shard_map/convert_element_type | solution.py:55
  1.0 0.1 copy.50
  1.1 0.8 %compare_and_fusion.7 = (pred[64]{0:T(512)(128)(4,1)S(1)}, s32[64]{0:T(128)S(1)}, pred[64]{0:T(512)(128)(4,1)S(1)}, s32[64]{0:T(128)S(1)}) fusion(s32[2,64]{1,0:T(2,128)} %param.19), kind=kLoop, calls=%fused_computation.109 | loop fusion | flops 768 | bytes 1152 | tf_op jit(solution)/shard_map/jit(_take)/and | solution.py:59
  1.9 0.7 %gather_fusion.1 = f32[64,2,128]{2,1,0:T(2,128)S(1)} fusion(f32[2,128,128]{1,0,2:T(2,128)S(1)} %copy.50, s32[1024]{0:T(1024)S(1)} %pad_clamp_fusion.6), kind=kCustom, calls=%fused_computation.2.clone | custom fusion | bytes 131328 | tf_op jit(solution)/shard_map/jit(_take)/gather | solution.py:58
  2.7 2.6 %collective-permute-start.8 = (f32[2,128,64]{2,1,0:T(8,128)S(1)}, f32[2,128,64]{2,1,0:T(8,128)S(1)}, u32[]{:S(2)}, u32[]{:S(2)}) collective-permute-start(f32[2,128,64]{2,1,0:T(8,128)S(1)} %select_bitcast_fusion), channel_id=1, source_target_pairs={{1,0},{2,1},{3,2},{4,3},{5,4},{6,5},{7,6},{8,7},{9,8},{10,9},{11,1... | collective-permute-start | bytes 196616 | tf_op jit(solution)/shard_map/ppermute | solution.py:61
  5.3 0.7 %gather_fusion = f32[64,2,128]{2,1,0:T(2,128)S(1)} fusion(f32[2,128,128]{1,0,2:T(2,128)S(1)} %copy.50, s32[1024]{0:T(1024)S(1)} %pad_clamp_fusion.7), kind=kCustom, calls=%fused_computation.clone | custom fusion | bytes 131328 | tf_op jit(solution)/shard_map/jit(_take)/gather | solution.py:59
  6.1 1.3 %collective-permute-start.7 = (f32[2,128,64]{2,1,0:T(8,128)S(1)}, f32[2,128,64]{2,1,0:T(8,128)S(1)}, u32[]{:S(2)}, u32[]{:S(2)}) collective-permute-start(f32[2,128,64]{2,1,0:T(8,128)S(1)} %select_bitcast_fusion.1), channel_id=1, source_target_pairs={{0,1},{1,2},{2,3},{3,4},{4,5},{5,6},{6,7},{7,8},{8,9},{9,10},{10,1... | collective-permute-start | bytes 196616 | tf_op jit(solution)/shard_map/ppermute | solution.py:60
  7.4 1.2 %collective-permute-start = (f32[2,128]{1,0:T(2,128)S(1)}, f32[2,128]{1,0:T(2,128)S(1)}, u32[]{:S(2)}, u32[]{:S(2)}) collective-permute-start(f32[2,128]{1,0:T(2,128)S(1)} %copy-done.1), channel_id=1, source_target_pairs={{0,1},{1,0},{2,3},{3,2},{4,5},{5,4},{6,7},{7,6},{8,9},{9,8},{10,11... | collective-permute-start | bytes 3080 | tf_op jit(solution)/shard_map/ppermute | solution.py:44
  8.7 2.5 %collective-permute-start.2 = (bf16[2,131,128]{2,1,0:T(8,128)(2,1)S(1)}, bf16[2,131,128]{2,1,0:T(8,128)(2,1)S(1)}, u32[]{:S(2)}, u32[]{:S(2)}) collective-permute-start(bf16[2,131,128]{2,1,0:T(8,128)(2,1)S(1)} %pad_maximum_fusion.5), channel_id=1, source_target_pairs={{0,16},{4,20},{8,24},{12,28},{16,0},{20,4},{24,8},{28,12},{1,17},{... | collective-permute-start | bytes 201224 | tf_op jit(solution)/shard_map/ppermute | solution.py:44
  11.3 2.7 %collective-permute-done.1 = f32[2,256]{1,0:T(2,128)S(1)} collective-permute-done((f32[2,256]{1,0:T(2,128)S(1)}, f32[2,256]{1,0:T(2,128)S(1)}, u32[]{:S(2)}, u32[]{:S(2)}) %collective-permute-start.1) | collective-permute-done | bytes 2080 | tf_op jit(solution)/shard_map/ppermute | solution.py:44
  14.0 2.2 %collective-permute-done.2 = bf16[2,131,128]{2,1,0:T(8,128)(2,1)S(1)} collective-permute-done((bf16[2,131,128]{2,1,0:T(8,128)(2,1)S(1)}, bf16[2,131,128]{2,1,0:T(8,128)(2,1)S(1)}, u32[]{:S(2)}, u32[]{:S(2)}) %collective-permute-start.2) | collective-permute-done | bytes 67104 | tf_op jit(solution)/shard_map/ppermute | solution.py:44
  16.4 2.2 %multiply_convert_fusion.5 = (bf16[128,512]{1,0:T(8,128)(2,1)S(1)}, bf16[128,512]{1,0:T(8,128)(2,1)S(1)}, bf16[128,512]{1,0:T(8,128)(2,1)S(1)}, bf16[128,512]{1,0:T(8,128)(2,1)S(1)}) fusion(f32[128]{0:T(128)S(1)} %get-tuple-element.62, f32[128]{0:T(128)S(1)} %get-tuple-element.61, f32[512]{0:T(512)S(1)} %bitcast.111, f32[512]{0:T(512)S(1)} %bitcast.108, ...), kind=kLoop, calls=%fused_computation.43 | loop fusion | flops 1310720 | bytes 530432 | tf_op jit(solution)/shard_map/convert_element_type | solution.py:31
  18.6 0.3 fusion.11
  18.9 0.3 convolution_add_fusion.1
  19.2 2.6 %collective-permute-done.3 = bf16[2,131,256]{2,1,0:T(8,128)(2,1)S(1)} collective-permute-done((bf16[2,131,256]{2,1,0:T(8,128)(2,1)S(1)}, bf16[2,131,256]{2,1,0:T(8,128)(2,1)S(1)}, u32[]{:S(2)}, u32[]{:S(2)}) %collective-permute-start.3) | collective-permute-done | bytes 134176 | tf_op jit(solution)/shard_map/ppermute | solution.py:44
  22.0 2.4 %multiply_convert_fusion.3 = (bf16[256,512]{1,0:T(8,128)(2,1)S(1)}, bf16[256,512]{1,0:T(8,128)(2,1)S(1)}) fusion(f32[256]{0:T(256)S(1)} %bitcast.117, f32[512]{0:T(512)S(1)} %bitcast.112, f32[256]{0:T(256)S(1)} %bitcast.116, f32[512]{0:T(512)S(1)} %bitcast.109), kind=kLoop, calls=%fused_computation.24 | loop fusion | flops 1310720 | bytes 530432 | tf_op jit(solution)/shard_map/convert_element_type | solution.py:31
  24.4 5.4 %collective-permute-done.4 = bf16[2,131,512]{2,1,0:T(8,128)(2,1)S(1)} collective-permute-done((bf16[2,131,512]{2,1,0:T(8,128)(2,1)S(1)}, bf16[2,131,512]{2,1,0:T(8,128)(2,1)S(1)}, u32[]{:S(2)}, u32[]{:S(2)}) %collective-permute-start.4) | collective-permute-done | bytes 268320 | tf_op jit(solution)/shard_map/ppermute | solution.py:44
  29.8 4.4 %multiply_convert_fusion.1 = (bf16[512,512]{1,0:T(8,128)(2,1)S(1)}, bf16[512,512]{1,0:T(8,128)(2,1)S(1)}) fusion(f32[512]{0:T(512)S(1)} %bitcast.115, f32[512]{0:T(512)S(1)} %bitcast.113, f32[512]{0:T(512)S(1)} %bitcast.114, f32[512]{0:T(512)S(1)} %bitcast.110), kind=kLoop, calls=%fused_computation.16 | loop fusion | flops 2621440 | bytes 1056768 | tf_op jit(solution)/shard_map/convert_element_type | solution.py:31
  34.3 0.4 fusion.1
  34.7 0.5 slice-done
  35.1 0.3 fusion
  35.8 0.1 copy.54
  36.0 0.7 %gather_fusion.7 = f32[128,2,128]{2,1,0:T(2,128)S(1)} fusion(f32[2,128,256]{1,0,2:T(2,128)S(1)} %copy.54, s32[1024]{0:T(1024)S(1)} %get-tuple-element.70), kind=kCustom, calls=%fused_computation.7.clone | custom fusion | bytes 262656 | tf_op jit(solution)/shard_map/jit(_take)/gather | solution.py:112
  36.8 0.7 %gather_fusion.6 = f32[128,2,128]{2,1,0:T(2,128)S(1)} fusion(f32[2,128,256]{1,0,2:T(2,128)S(1)} %copy.54, s32[1024]{0:T(1024)S(1)} %get-tuple-element.71), kind=kCustom, calls=%fused_computation.6.clone | custom fusion | bytes 262656 | tf_op jit(solution)/shard_map/jit(_take)/gather | solution.py:112
  37.7 0.8 %gather_fusion.5 = f32[128,2,128]{2,1,0:T(2,128)S(1)} fusion(f32[2,128,256]{1,0,2:T(2,128)S(1)} %copy.54, s32[1024]{0:T(1024)S(1)} %get-tuple-element.72), kind=kCustom, calls=%fused_computation.5.clone | custom fusion | bytes 262656 | tf_op jit(solution)/shard_map/jit(_take)/gather | solution.py:112
  38.5 0.7 %gather_fusion.4 = f32[128,2,128]{2,1,0:T(2,128)S(1)} fusion(f32[2,128,256]{1,0,2:T(2,128)S(1)} %copy.54, s32[1024]{0:T(1024)S(1)} %get-tuple-element.73), kind=kCustom, calls=%fused_computation.4.clone | custom fusion | bytes 262656 | tf_op jit(solution)/shard_map/jit(_take)/gather | solution.py:112
  39.4 0.7 %gather_fusion.3 = f32[128,2,128]{2,1,0:T(2,128)S(1)} fusion(f32[2,128,256]{1,0,2:T(2,128)S(1)} %copy.54, s32[1024]{0:T(1024)S(1)} %get-tuple-element.74), kind=kCustom, calls=%fused_computation.3.clone | custom fusion | bytes 262656 | tf_op jit(solution)/shard_map/jit(_take)/gather | solution.py:112
  40.3 0.7 %gather_fusion.2 = f32[128,2,128]{2,1,0:T(2,128)S(1)} fusion(f32[2,128,256]{1,0,2:T(2,128)S(1)} %copy.54, s32[1024]{0:T(1024)S(1)} %get-tuple-element.75), kind=kCustom, calls=%fused_computation.1.clone | custom fusion | bytes 262656 | tf_op jit(solution)/shard_map/jit(_take)/gather | solution.py:112
  41.1 1.2 %collective-permute-done.5 = f32[2,128,256]{2,1,0:T(8,128)S(1)} collective-permute-done((f32[2,128,256]{2,1,0:T(8,128)S(1)}, f32[2,128,256]{2,1,0:T(8,128)S(1)}, u32[]{:S(2)}, u32[]{:S(2)}) %collective-permute-start.5) | collective-permute-done | bytes 262176 | tf_op jit(solution)/shard_map/ppermute | solution.py:44
  42.4 2.2 %collective-permute-start.6 = (f32[2,128,128]{2,1,0:T(8,128)S(1)}, f32[2,128,128]{2,1,0:T(8,128)S(1)}, u32[]{:S(2)}, u32[]{:S(2)}) collective-permute-start(f32[2,128,128]{2,1,0:T(8,128)S(1)} %slice_select_fusion), channel_id=1, source_target_pairs={{0,1},{1,0},{2,3},{3,2},{4,5},{5,4},{6,7},{7,6},{8,9},{9,8},{10,11... | collective-permute-start | bytes 393224 | tf_op jit(solution)/shard_map/ppermute | solution.py:44
  44.6 0.9 %collective-permute-done.6 = f32[2,128,128]{2,1,0:T(8,128)S(1)} collective-permute-done((f32[2,128,128]{2,1,0:T(8,128)S(1)}, f32[2,128,128]{2,1,0:T(8,128)S(1)}, u32[]{:S(2)}, u32[]{:S(2)}) %collective-permute-start.6) | collective-permute-done | bytes 131104 | tf_op jit(solution)/shard_map/ppermute | solution.py:44
  45.6 0.7 %pad_maximum_fusion.4 = f32[2,128,128]{2,1,0:T(8,128)} fusion(f32[1,128,128]{2,1,0:T(8,128)S(1)} %get-tuple-element.28, f32[1,128,128]{2,1,0:T(8,128)S(1)} %get-tuple-element.27), kind=kLoop, calls=%fused_computation.49 | loop fusion | flops 32768 | bytes 262144 | tf_op jit(solution)/shard_map/stack | solution.py:123
  (64 shorter events, 1.8 us)
Async XLA Ops:
  0.0 7.4 %copy-start.1 = (f32[2,128]{1,0:T(2,128)S(1)}, f32[2,128]{1,0:T(2,128)}, u32[]{:S(2)}) copy-start(f32[2,128]{1,0:T(2,128)} %param.14) | copy-start | bytes 3076
  1.0 10.1 %copy-start.3 = (s32[6,128]{1,0:T(8,128)S(1)}, s32[6,128]{1,0:T(8,128)}, u32[]{:S(2)}) copy-start(s32[6,128]{1,0:T(8,128)} %param.18) | copy-start | bytes 9220
  1.0 10.2 %copy-start.2 = (f32[6,128]{1,0:T(8,128)S(1)}, f32[6,128]{1,0:T(8,128)}, u32[]{:S(2)}) copy-start(f32[6,128]{1,0:T(8,128)} %param.17) | copy-start | bytes 9220
  2.7 33.0 %collective-permute-start.8 = (f32[2,128,64]{2,1,0:T(8,128)S(1)}, f32[2,128,64]{2,1,0:T(8,128)S(1)}, u32[]{:S(2)}, u32[]{:S(2)}) collective-permute-start(f32[2,128,64]{2,1,0:T(8,128)S(1)} %select_bitcast_fusion), channel_id=1, source_target_pairs={{1,0},{2,1},{3,2},{4,3},{5,4},{6,5},{7,6},{8,7},{9,8},{10,9},{11,1... | collective-permute-start | bytes 196616 | tf_op jit(solution)/shard_map/ppermute | solution.py:61
  6.1 29.6 %collective-permute-start.7 = (f32[2,128,64]{2,1,0:T(8,128)S(1)}, f32[2,128,64]{2,1,0:T(8,128)S(1)}, u32[]{:S(2)}, u32[]{:S(2)}) collective-permute-start(f32[2,128,64]{2,1,0:T(8,128)S(1)} %select_bitcast_fusion.1), channel_id=1, source_target_pairs={{0,1},{1,2},{2,3},{3,4},{4,5},{5,6},{6,7},{7,8},{8,9},{9,10},{10,1... | collective-permute-start | bytes 196616 | tf_op jit(solution)/shard_map/ppermute | solution.py:60
  7.4 3.8 %collective-permute-start = (f32[2,128]{1,0:T(2,128)S(1)}, f32[2,128]{1,0:T(2,128)S(1)}, u32[]{:S(2)}, u32[]{:S(2)}) collective-permute-start(f32[2,128]{1,0:T(2,128)S(1)} %copy-done.1), channel_id=1, source_target_pairs={{0,1},{1,0},{2,3},{3,2},{4,5},{5,4},{6,7},{7,6},{8,9},{9,8},{10,11... | collective-permute-start | bytes 3080 | tf_op jit(solution)/shard_map/ppermute | solution.py:44
  8.7 7.6 %collective-permute-start.2 = (bf16[2,131,128]{2,1,0:T(8,128)(2,1)S(1)}, bf16[2,131,128]{2,1,0:T(8,128)(2,1)S(1)}, u32[]{:S(2)}, u32[]{:S(2)}) collective-permute-start(bf16[2,131,128]{2,1,0:T(8,128)(2,1)S(1)} %pad_maximum_fusion.5), channel_id=1, source_target_pairs={{0,16},{4,20},{8,24},{12,28},{16,0},{20,4},{24,8},{28,12},{1,17},{... | collective-permute-start | bytes 201224 | tf_op jit(solution)/shard_map/ppermute | solution.py:44
  11.2 2.8 %collective-permute-start.1 = (f32[2,256]{1,0:T(2,128)S(1)}, f32[2,256]{1,0:T(2,128)S(1)}, u32[]{:S(2)}, u32[]{:S(2)}) collective-permute-start(f32[2,256]{1,0:T(2,128)S(1)} %maximum_select_fusion.1), channel_id=1, source_target_pairs={{0,2},{1,3},{2,0},{3,1},{4,6},{5,7},{6,4},{7,5},{8,10},{9,11},{10,... | collective-permute-start | bytes 6152 | tf_op jit(solution)/shard_map/ppermute | solution.py:44
  16.3 5.6 %collective-permute-start.3 = (bf16[2,131,256]{2,1,0:T(8,128)(2,1)S(1)}, bf16[2,131,256]{2,1,0:T(8,128)(2,1)S(1)}, u32[]{:S(2)}, u32[]{:S(2)}) collective-permute-start(bf16[2,131,256]{2,1,0:T(8,128)(2,1)S(1)} %pad_maximum_fusion.3), channel_id=1, source_target_pairs={{0,8},{4,12},{8,0},{12,4},{16,24},{20,28},{24,16},{28,20},{1,9},{5... | collective-permute-start | bytes 402440 | tf_op jit(solution)/shard_map/ppermute | solution.py:44
  21.8 12.4 %copy-start = (bf16[2,131,256]{2,1,0:T(8,128)(2,1)}, bf16[2,131,256]{2,1,0:T(8,128)(2,1)S(1)}, u32[]{:S(2)}) copy-start(bf16[2,131,256]{2,1,0:T(8,128)(2,1)S(1)} %collective-permute-done.3) | copy-start | bytes 402436
  21.9 7.9 %collective-permute-start.4 = (bf16[2,131,512]{2,1,0:T(8,128)(2,1)S(1)}, bf16[2,131,512]{2,1,0:T(8,128)(2,1)S(1)}, u32[]{:S(2)}, u32[]{:S(2)}) collective-permute-start(bf16[2,131,512]{2,1,0:T(8,128)(2,1)S(1)} %pad_maximum_fusion), channel_id=1, source_target_pairs={{0,4},{4,0},{8,12},{12,8},{16,20},{20,16},{24,28},{28,24},{1,5},{5... | collective-permute-start | bytes 804872 | tf_op jit(solution)/shard_map/ppermute | solution.py:44
  34.2 0.9 %slice-start = ((bf16[2,131,256]{2,1,0:T(8,128)(2,1)}), bf16[2,128,256]{2,1,0:T(8,128)(2,1)S(1)}, s32[]{:S(2)}) async-start(bf16[2,131,256]{2,1,0:T(8,128)(2,1)} %copy-done), calls=%async_computation | async-start | bytes 262144 | tf_op jit(solution)/shard_map/slice | solution.py:86
  35.6 6.7 %collective-permute-start.5 = (f32[2,128,256]{2,1,0:T(8,128)S(1)}, f32[2,128,256]{2,1,0:T(8,128)S(1)}, u32[]{:S(2)}, u32[]{:S(2)}) collective-permute-start(f32[2,128,256]{2,1,0:T(8,128)S(1)} %broadcast_select_fusion), channel_id=1, source_target_pairs={{0,2},{1,3},{2,0},{3,1},{4,6},{5,7},{6,4},{7,5},{8,10},{9,11},{10,... | collective-permute-start | bytes 786440 | tf_op jit(solution)/shard_map/ppermute | solution.py:44
  42.3 3.2 %copy-start.4 = (f32[128]{0:T(128)S(1)}, f32[128]{0:T(128)}, u32[]{:S(2)}) copy-start(f32[128]{0:T(128)} %param.16) | copy-start | bytes 1540
  42.3 3.2 %copy-start.5 = (f32[128]{0:T(128)S(1)}, f32[128]{0:T(128)}, u32[]{:S(2)}) copy-start(f32[128]{0:T(128)} %param.15) | copy-start | bytes 1540
  42.4 3.2 %collective-permute-start.6 = (f32[2,128,128]{2,1,0:T(8,128)S(1)}, f32[2,128,128]{2,1,0:T(8,128)S(1)}, u32[]{:S(2)}, u32[]{:S(2)}) collective-permute-start(f32[2,128,128]{2,1,0:T(8,128)S(1)} %slice_select_fusion), channel_id=1, source_target_pairs={{0,1},{1,0},{2,3},{3,2},{4,5},{5,4},{6,7},{7,6},{8,9},{9,8},{10,11... | collective-permute-start | bytes 393224 | tf_op jit(solution)/shard_map/ppermute | solution.py:44

commit v3 on v2

--- a/solution.py
+++ b/solution.py
@@ -55,13 +55,28 @@
     section_half = section_field.astype(jnp.bfloat16)
     where_in_group = lax.axis_index("grp")
 
-    to_prev = jnp.take(section_field, send_list[1], axis=2)
-    to_next = jnp.take(section_field, send_list[0], axis=2)
-    from_prev = lax.ppermute(to_next, ALL, [(i, i + 1) for i in range(devices - 1)])
-    from_next = lax.ppermute(to_prev, ALL, [(i + 1, i) for i in range(devices - 1)])
+    me = lax.axis_index(ALL)
+    odd = (me % 2) == 1
+    lists = jnp.take(section_field, jnp.concatenate([send_list[1], send_list[0]]), axis=2)
+    halo_width = send_list.shape[1]
+    to_prev = lists[:, :, :halo_width]
+    to_next = lists[:, :, halo_width:]
+    paired = jnp.where(odd, to_prev, to_next)
+    crossed = jnp.where(odd, to_next, to_prev)
+    crossing = [(i, i + 1) for i in range(1, devices - 1, 2)]
+    crossing += [(i, i - 1) for i in range(2, devices, 2)]
+    from_crossed = lax.ppermute(crossed, ALL, crossing)
 
-    targets = positions
-    mask = 1
+    coded = positions.reshape(2, rows_here // halo_width, halo_width)
+    first = exchange(jnp.concatenate([paired, coded], axis=1), "grp", 1)
+    from_paired = first[:, :members]
+    other = first[:, members:].reshape(2, rows_here)
+    targets = jnp.where(
+        odd,
+        jnp.concatenate([other, positions], axis=1),
+        jnp.concatenate([positions, other], axis=1),
+    )
+    mask = 2
     while mask < group:
         other = exchange(targets, "grp", mask)
         upper = (where_in_group & mask) != 0
@@ -72,6 +87,8 @@
         )
         mask *= 2
     width = targets.shape[1]
+    from_prev = jnp.where(odd, from_paired, from_crossed)
+    from_next = jnp.where(odd, from_crossed, from_paired)
 
     pieces = jnp.stack(bf16_pieces(positions), axis=1)
     payload = jnp.concatenate([section_half, pieces], axis=1)
@@ -107,10 +124,15 @@
     imag_part = partial[1]
 
     local_buffer = jnp.concatenate([section_field, from_prev, from_next], axis=2)
-    coupled = jnp.zeros((2, members, rows_here), jnp.float32)
-    for neighbour_slot in range(kappa.shape[0]):
-        picked = jnp.take(local_buffer, neighbours[neighbour_slot], axis=2)
-        coupled = coupled + kappa[neighbour_slot] * picked
+    places = local_buffer.shape[2]
+    hit = neighbours[:, None, :] == lax.broadcasted_iota(jnp.int32, (1, places, 1), 1)
+    weights = jnp.sum(jnp.where(hit, kappa[:, None, :], 0.0), axis=0)
+    coupled = jnp.dot(
+        local_buffer.reshape(2 * members, places),
+        weights,
+        precision=lax.Precision.HIGHEST,
+        preferred_element_type=jnp.float32,
+    ).reshape(2, members, rows_here)
     real_field = section_field[0]
     imag_field = section_field[1]
     modulus = real_field * real_field + imag_field * imag_field

time: 46.5 us -> 43.2 us (0.929)
  the two profiles are of different devices: /device:TPU:31 before, /device:TPU:0 now
where the time goes in v3:
time: 43.2 us; the launch traced here: 43 us
  waiting for transfers between devices  17.3 us (40%)
  other arithmetic  11.6 us (27%)
  starting transfers between devices  9.67 us (22%)
  local copies, waits for them, and re-layouts  2.43 us (6%)
  matrix products  1.67 us (4%)
    ppermute x7, waiting for transfers between devices, exchange(): return lax.ppermute(value, axis, [(i, i ^ mask) for i in range(count)])  17.3 us
    convert_element_type x3, other arithmetic, kernel_table(): cosine = (scaled * jnp.cos(phase)).astype(jnp.bfloat16)  9.04 us
    ppermute x7, starting transfers between devices, exchange(): return lax.ppermute(value, axis, [(i, i ^ mask) for i in range(count)])  9 us
    dot_general x4, matrix products, block_product(): return jnp.dot(flat, kernel, preferred_element_type=jnp.float32)  1.29 us
    convert_element_type x1, other arithmetic, local(): section_half = section_field.astype(jnp.bfloat16)  1 us
  transfers between devices with their start and end apart: 8, of which 5 were waited for; matrix products, arithmetic and copies ran while one was open for 26% of the time, Pallas kernels for 0%

profile of v3, /device:TPU:0, one launch (start us, length us, event | category | flops | bytes accessed | tf_op | source)
XLA Modules:
  0.0 43.0 jit_solution(8566129215172708227)
XLA Ops:
  0.0 1.0 %fusion.35 = (bf16[2,128,128]{2,1,0:T(8,128)(2,1)S(1)}, f32[2,128,128]{2,1,0:T(8,128)S(1)}) fusion(f32[2,128,128]{2,1,0:T(8,128)} %param.8, f32[2,128,128]{2,1,0:T(8,128)} %param.9), kind=kLoop, calls=%fused_computation.106 | loop fusion | flops 98304 | bytes 458752 | tf_op jit(solution)/shard_map/convert_element_type | solution.py:55
  1.0 0.1 copy.24
  1.1 0.8 %slice_bitcast_fusion.9 = (s32[64]{0:T(128)S(1)}, s32[64,1]{0,1:T(1,128)S(1)}, s32[64,1]{0,1:T(1,128)S(1)}, s32[64]{0:T(128)S(1)}) fusion(s32[2,64]{1,0:T(2,128)} %param.15), kind=kLoop, calls=%fused_computation.101 | loop fusion | bytes 1536 | tf_op jit(solution)/shard_map/concatenate | solution.py:60
  2.0 0.7 %gather_fusion = f32[128,2,128]{2,1,0:T(2,128)S(1)} fusion(f32[2,128,128]{1,0,2:T(2,128)S(1)} %copy.24, s32[1024]{0:T(1024)S(1)} %pad_clamp_fusion), kind=kCustom, calls=%fused_computation | custom fusion | bytes 262656 | tf_op jit(solution)/shard_map/jit(_take)/gather | solution.py:60
  2.7 0.1 copy.25
  2.9 0.1 compare_and_fusion
  3.0 0.1 slice_select_fusion.4
  3.1 0.7 %collective-permute-start.7 = (f32[2,128,64]{2,1,0:T(8,128)S(1)}, f32[2,128,64]{2,1,0:T(8,128)S(1)}, u32[]{:S(2)}, u32[]{:S(2)}) collective-permute-start(f32[2,128,64]{2,1,0:T(8,128)S(1)} %get-tuple-element.14), channel_id=1, source_target_pairs={{1,2},{3,4},{5,6},{7,8},{9,10},{11,12},{13,14},{15,16},{17,18},{19... | collective-permute-start | bytes 196616 | tf_op jit(solution)/shard_map/ppermute | solution.py:68
  3.8 0.1 reshape.187
  3.9 4.4 %collective-permute-start = (f32[2,130,64]{2,1,0:T(8,128)S(1)}, f32[2,130,64]{2,1,0:T(8,128)S(1)}, u32[]{:S(2)}, u32[]{:S(2)}) collective-permute-start(f32[2,130,64]{2,1,0:T(8,128)S(1)} %pad_maximum_fusion.3), channel_id=1, source_target_pairs={{0,1},{1,0},{2,3},{3,2},{4,5},{5,4},{6,7},{7,6},{8,9},{9,8},{10,11... | collective-permute-start | bytes 199688 | tf_op jit(solution)/shard_map/ppermute | solution.py:44
  8.3 2.8 %collective-permute-start.2 = (bf16[2,131,128]{2,1,0:T(8,128)(2,1)S(1)}, bf16[2,131,128]{2,1,0:T(8,128)(2,1)S(1)}, u32[]{:S(2)}, u32[]{:S(2)}) collective-permute-start(bf16[2,131,128]{2,1,0:T(8,128)(2,1)S(1)} %pad_maximum_fusion.6), channel_id=1, source_target_pairs={{0,16},{4,20},{8,24},{12,28},{16,0},{20,4},{24,8},{28,12},{1,17},{... | collective-permute-start | bytes 201224 | tf_op jit(solution)/shard_map/ppermute | solution.py:44
  11.2 0.1 select_reduce_fusion
  11.3 0.1 reshape.188
  11.4 1.3 %collective-permute-start.1 = (f32[2,256]{1,0:T(2,128)S(1)}, f32[2,256]{1,0:T(2,128)S(1)}, u32[]{:S(2)}, u32[]{:S(2)}) collective-permute-start(f32[2,256]{1,0:T(2,128)S(1)} %maximum_select_fusion.1), channel_id=1, source_target_pairs={{0,2},{1,3},{2,0},{3,1},{4,6},{5,7},{6,4},{7,5},{8,10},{9,11},{10,... | collective-permute-start | bytes 6152 | tf_op jit(solution)/shard_map/ppermute | solution.py:44
  12.7 4.1 %collective-permute-done.2 = bf16[2,131,128]{2,1,0:T(8,128)(2,1)S(1)} collective-permute-done((bf16[2,131,128]{2,1,0:T(8,128)(2,1)S(1)}, bf16[2,131,128]{2,1,0:T(8,128)(2,1)S(1)}, u32[]{:S(2)}, u32[]{:S(2)}) %collective-permute-start.2) | collective-permute-done | bytes 67104 | tf_op jit(solution)/shard_map/ppermute | solution.py:44
  16.8 0.3 collective-permute-start.3
  17.1 2.2 %multiply_convert_fusion.5 = (bf16[128,512]{1,0:T(8,128)(2,1)S(1)}, bf16[128,512]{1,0:T(8,128)(2,1)S(1)}, bf16[128,512]{1,0:T(8,128)(2,1)S(1)}, bf16[128,512]{1,0:T(8,128)(2,1)S(1)}) fusion(f32[128]{0:T(128)S(1)} %get-tuple-element.32, f32[128]{0:T(128)S(1)} %get-tuple-element.31, f32[512]{0:T(512)S(1)} %bitcast.63, f32[512]{0:T(512)S(1)} %bitcast.60, ...), kind=kLoop, calls=%fused_computation.38 | loop fusion | flops 1310720 | bytes 530432 | tf_op jit(solution)/shard_map/convert_element_type | solution.py:31
  19.3 0.3 fusion.11
  19.6 0.3 convolution_add_fusion.1
  19.9 2.0 %collective-permute-done.3 = bf16[2,131,256]{2,1,0:T(8,128)(2,1)S(1)} collective-permute-done((bf16[2,131,256]{2,1,0:T(8,128)(2,1)S(1)}, bf16[2,131,256]{2,1,0:T(8,128)(2,1)S(1)}, u32[]{:S(2)}, u32[]{:S(2)}) %collective-permute-start.3) | collective-permute-done | bytes 134176 | tf_op jit(solution)/shard_map/ppermute | solution.py:44
  22.0 2.4 %multiply_convert_fusion.3 = (bf16[256,512]{1,0:T(8,128)(2,1)S(1)}, bf16[256,512]{1,0:T(8,128)(2,1)S(1)}) fusion(f32[256]{0:T(256)S(1)} %bitcast.69, f32[512]{0:T(512)S(1)} %bitcast.64, f32[256]{0:T(256)S(1)} %bitcast.68, f32[512]{0:T(512)S(1)} %bitcast.61), kind=kLoop, calls=%fused_computation.19 | loop fusion | flops 1310720 | bytes 530432 | tf_op jit(solution)/shard_map/convert_element_type | solution.py:31
  24.4 4.1 %collective-permute-done.4 = bf16[2,131,512]{2,1,0:T(8,128)(2,1)S(1)} collective-permute-done((bf16[2,131,512]{2,1,0:T(8,128)(2,1)S(1)}, bf16[2,131,512]{2,1,0:T(8,128)(2,1)S(1)}, u32[]{:S(2)}, u32[]{:S(2)}) %collective-permute-start.4) | collective-permute-done | bytes 268320 | tf_op jit(solution)/shard_map/ppermute | solution.py:44
  28.5 4.4 %multiply_convert_fusion.1 = (bf16[512,512]{1,0:T(8,128)(2,1)S(1)}, bf16[512,512]{1,0:T(8,128)(2,1)S(1)}) fusion(f32[512]{0:T(512)S(1)} %bitcast.67, f32[512]{0:T(512)S(1)} %bitcast.65, f32[512]{0:T(512)S(1)} %bitcast.66, f32[512]{0:T(512)S(1)} %bitcast.62), kind=kLoop, calls=%fused_computation.9 | loop fusion | flops 2621440 | bytes 1056768 | tf_op jit(solution)/shard_map/convert_element_type | solution.py:31
  33.0 0.4 fusion.1
  33.5 0.5 %slice-done = bf16[2,128,256]{2,1,0:T(8,128)(2,1)S(1)} async-done(((bf16[2,131,256]{2,1,0:T(8,128)(2,1)}), bf16[2,128,256]{2,1,0:T(8,128)(2,1)S(1)}, s32[]{:S(2)}) %slice-start) | async-done | bytes 131096 | tf_op jit(solution)/shard_map/slice | solution.py:103
  33.9 0.3 fusion
  34.2 0.1 fusion.10
  34.5 0.1 pad_maximum_fusion.2
  34.6 6.2 %collective-permute-done.5 = f32[2,128,256]{2,1,0:T(8,128)S(1)} collective-permute-done((f32[2,128,256]{2,1,0:T(8,128)S(1)}, f32[2,128,256]{2,1,0:T(8,128)S(1)}, u32[]{:S(2)}, u32[]{:S(2)}) %collective-permute-start.5) | collective-permute-done | bytes 262176 | tf_op jit(solution)/shard_map/ppermute | solution.py:44
  41.0 0.4 fusion.39
  41.3 1.0 %collective-permute-done.6 = f32[2,128,128]{2,1,0:T(8,128)S(1)} collective-permute-done((f32[2,128,128]{2,1,0:T(8,128)S(1)}, f32[2,128,128]{2,1,0:T(8,128)S(1)}, u32[]{:S(2)}, u32[]{:S(2)}) %collective-permute-start.6) | collective-permute-done | bytes 131104 | tf_op jit(solution)/shard_map/ppermute | solution.py:44
  42.4 0.7 %pad_maximum_fusion.5 = f32[2,128,128]{2,1,0:T(8,128)} fusion(f32[1,128,128]{2,1,0:T(8,128)S(1)} %get-tuple-element.10, f32[1,128,128]{2,1,0:T(8,128)S(1)} %get-tuple-element.9), kind=kLoop, calls=%fused_computation.45 | loop fusion | flops 32768 | bytes 262144 | tf_op jit(solution)/shard_map/stack | solution.py:145
  (49 shorter events, 0.7 us)
Async XLA Ops:
  0.0 3.7 %copy-start.1 = (f32[2,128]{1,0:T(2,128)S(1)}, f32[2,128]{1,0:T(2,128)}, u32[]{:S(2)}) copy-start(f32[2,128]{1,0:T(2,128)} %param.10) | copy-start | bytes 3076
  1.0 10.1 %copy-start.2 = (f32[6,128]{1,0:T(8,128)S(1)}, f32[6,128]{1,0:T(8,128)}, u32[]{:S(2)}) copy-start(f32[6,128]{1,0:T(8,128)} %param.13) | copy-start | bytes 9220
  1.0 10.1 %copy-start.3 = (s32[6,128]{1,0:T(8,128)S(1)}, s32[6,128]{1,0:T(8,128)}, u32[]{:S(2)}) copy-start(s32[6,128]{1,0:T(8,128)} %param.14) | copy-start | bytes 9220
  3.1 31.4 %collective-permute-start.7 = (f32[2,128,64]{2,1,0:T(8,128)S(1)}, f32[2,128,64]{2,1,0:T(8,128)S(1)}, u32[]{:S(2)}, u32[]{:S(2)}) collective-permute-start(f32[2,128,64]{2,1,0:T(8,128)S(1)} %get-tuple-element.14), channel_id=1, source_target_pairs={{1,2},{3,4},{5,6},{7,8},{9,10},{11,12},{13,14},{15,16},{17,18},{19... | collective-permute-start | bytes 196616 | tf_op jit(solution)/shard_map/ppermute | solution.py:68
  3.9 7.4 %collective-permute-start = (f32[2,130,64]{2,1,0:T(8,128)S(1)}, f32[2,130,64]{2,1,0:T(8,128)S(1)}, u32[]{:S(2)}, u32[]{:S(2)}) collective-permute-start(f32[2,130,64]{2,1,0:T(8,128)S(1)} %pad_maximum_fusion.3), channel_id=1, source_target_pairs={{0,1},{1,0},{2,3},{3,2},{4,5},{5,4},{6,7},{7,6},{8,9},{9,8},{10,11... | collective-permute-start | bytes 199688 | tf_op jit(solution)/shard_map/ppermute | solution.py:44
  8.3 8.4 %collective-permute-start.2 = (bf16[2,131,128]{2,1,0:T(8,128)(2,1)S(1)}, bf16[2,131,128]{2,1,0:T(8,128)(2,1)S(1)}, u32[]{:S(2)}, u32[]{:S(2)}) collective-permute-start(bf16[2,131,128]{2,1,0:T(8,128)(2,1)S(1)} %pad_maximum_fusion.6), channel_id=1, source_target_pairs={{0,16},{4,20},{8,24},{12,28},{16,0},{20,4},{24,8},{28,12},{1,17},{... | collective-permute-start | bytes 201224 | tf_op jit(solution)/shard_map/ppermute | solution.py:44
  11.4 5.7 %collective-permute-start.1 = (f32[2,256]{1,0:T(2,128)S(1)}, f32[2,256]{1,0:T(2,128)S(1)}, u32[]{:S(2)}, u32[]{:S(2)}) collective-permute-start(f32[2,256]{1,0:T(2,128)S(1)} %maximum_select_fusion.1), channel_id=1, source_target_pairs={{0,2},{1,3},{2,0},{3,1},{4,6},{5,7},{6,4},{7,5},{8,10},{9,11},{10,... | collective-permute-start | bytes 6152 | tf_op jit(solution)/shard_map/ppermute | solution.py:44
  16.8 5.1 %collective-permute-start.3 = (bf16[2,131,256]{2,1,0:T(8,128)(2,1)S(1)}, bf16[2,131,256]{2,1,0:T(8,128)(2,1)S(1)}, u32[]{:S(2)}, u32[]{:S(2)}) collective-permute-start(bf16[2,131,256]{2,1,0:T(8,128)(2,1)S(1)} %pad_maximum_fusion.4), channel_id=1, source_target_pairs={{0,8},{4,12},{8,0},{12,4},{16,24},{20,28},{24,16},{28,20},{1,9},{5... | collective-permute-start | bytes 402440 | tf_op jit(solution)/shard_map/ppermute | solution.py:44
  21.9 11.1 %copy-start = (bf16[2,131,256]{2,1,0:T(8,128)(2,1)}, bf16[2,131,256]{2,1,0:T(8,128)(2,1)S(1)}, u32[]{:S(2)}) copy-start(bf16[2,131,256]{2,1,0:T(8,128)(2,1)S(1)} %collective-permute-done.3) | copy-start | bytes 402436
  21.9 6.6 %collective-permute-start.4 = (bf16[2,131,512]{2,1,0:T(8,128)(2,1)S(1)}, bf16[2,131,512]{2,1,0:T(8,128)(2,1)S(1)}, u32[]{:S(2)}, u32[]{:S(2)}) collective-permute-start(bf16[2,131,512]{2,1,0:T(8,128)(2,1)S(1)} %pad_maximum_fusion), channel_id=1, source_target_pairs={{0,4},{4,0},{8,12},{12,8},{16,20},{20,16},{24,28},{28,24},{1,5},{5... | collective-permute-start | bytes 804872 | tf_op jit(solution)/shard_map/ppermute | solution.py:44
  33.0 0.9 %slice-start = ((bf16[2,131,256]{2,1,0:T(8,128)(2,1)}), bf16[2,128,256]{2,1,0:T(8,128)(2,1)S(1)}, s32[]{:S(2)}) async-start(bf16[2,131,256]{2,1,0:T(8,128)(2,1)} %copy-done), calls=%async_computation | async-start | bytes 262144 | tf_op jit(solution)/shard_map/slice | solution.py:103
  34.4 6.4 %collective-permute-start.5 = (f32[2,128,256]{2,1,0:T(8,128)S(1)}, f32[2,128,256]{2,1,0:T(8,128)S(1)}, u32[]{:S(2)}, u32[]{:S(2)}) collective-permute-start(f32[2,128,256]{2,1,0:T(8,128)S(1)} %broadcast_select_fusion), channel_id=1, source_target_pairs={{0,2},{1,3},{2,0},{3,1},{4,6},{5,7},{6,4},{7,5},{8,10},{9,11},{10,... | collective-permute-start | bytes 786440 | tf_op jit(solution)/shard_map/ppermute | solution.py:44
  34.6 7.7 %copy-start.4 = (f32[128]{0:T(128)S(1)}, f32[128]{0:T(128)}, u32[]{:S(2)}) copy-start(f32[128]{0:T(128)} %param.12) | copy-start | bytes 1540
  34.6 7.7 %copy-start.5 = (f32[128]{0:T(128)S(1)}, f32[128]{0:T(128)}, u32[]{:S(2)}) copy-start(f32[128]{0:T(128)} %param.11) | copy-start | bytes 1540
  40.9 1.4 %collective-permute-start.6 = (f32[2,128,128]{2,1,0:T(8,128)S(1)}, f32[2,128,128]{2,1,0:T(8,128)S(1)}, u32[]{:S(2)}, u32[]{:S(2)}) collective-permute-start(f32[2,128,128]{2,1,0:T(8,128)S(1)} %slice_select_fusion.2), channel_id=1, source_target_pairs={{0,1},{1,0},{2,3},{3,2},{4,5},{5,4},{6,7},{7,6},{8,9},{9,8},{10,11... | collective-permute-start | bytes 393224 | tf_op jit(solution)/shard_map/ppermute | solution.py:44

commit v4 on v3

--- a/solution.py
+++ b/solution.py
@@ -57,7 +57,14 @@
 
     me = lax.axis_index(ALL)
     odd = (me % 2) == 1
-    lists = jnp.take(section_field, jnp.concatenate([send_list[1], send_list[0]]), axis=2)
+    listed = jnp.concatenate([send_list[1], send_list[0]])
+    pick = (lax.broadcasted_iota(jnp.int32, (rows_here, 1), 0) == listed[None, :]).astype(jnp.float32)
+    lists = jnp.dot(
+        section_field.reshape(2 * members, rows_here),
+        pick,
+        precision=lax.Precision.HIGHEST,
+        preferred_element_type=jnp.float32,
+    ).reshape(2, members, -1)
     halo_width = send_list.shape[1]
     to_prev = lists[:, :, :halo_width]
     to_next = lists[:, :, halo_width:]
@@ -110,16 +117,16 @@
         ]
     )
 
-    mask = group // 2
-    while mask >= 1:
-        half = partial.shape[2] // 2
-        lower = partial[:, :, :half]
-        higher = partial[:, :, half:]
+    count = group
+    mask = 1
+    while mask < group:
+        split = partial.reshape(2, members, count // 2, 2, rows_here)
         upper = (where_in_group & mask) != 0
-        keep = jnp.where(upper, higher, lower)
-        give = jnp.where(upper, lower, higher)
-        partial = keep + exchange(give, "grp", mask)
-        mask //= 2
+        keep = jnp.where(upper, split[:, :, :, 1], split[:, :, :, 0])
+        give = jnp.where(upper, split[:, :, :, 0], split[:, :, :, 1])
+        partial = (keep + exchange(give, "grp", mask)).reshape(2, members, -1)
+        count //= 2
+        mask *= 2
     real_part = partial[0]
     imag_part = partial[1]
 

time: 43.2 us -> 42 us (0.972)
  waiting for transfers between devices: 17.3 us -> 13.1 us
  starting transfers between devices: 9.67 us -> 12.1 us
  local copies, waits for them, and re-layouts: 2.43 us -> 2.91 us
    ppermute x7, waiting for transfers between devices: 17.3 us -> 13.1 us  [exchange(): return lax.ppermute(value, axis, [(i, i ^ mask) for i in range(count)])]
    ppermute x7, starting transfers between devices: 9 us -> 11.4 us  [exchange(): return lax.ppermute(value, axis, [(i, i ^ mask) for i in range(count)])]
    gather x2 -> x0, local copies, waits for them, and re-layouts: 0.84 us -> none  [local(): jnp.take(section_field, jnp.concatenate([send_list[1], send_list[0]]), ax...]
    reshape x1 -> x2, local copies, waits for them, and re-layouts: 0.08 us -> 0.87 us  [local(): coded = positions.reshape(2, rows_here // halo_width, halo_width)]
    concatenate x1 -> x0, local copies, waits for them, and re-layouts: 0.76 us -> none  [local(): jnp.concatenate([send_list[1], send_list[0]])]
    squeeze x0 -> x1, local copies, waits for them, and re-layouts: none -> 0.76 us  [local(): listed = jnp.concatenate([send_list[1], send_list[0]])]
  transfers between devices with their start and end apart: 8 -> 8, of which waited for: 5 -> 5; matrix products, arithmetic and copies ran while one was open for 26% -> 31% of each run, Pallas kernels for 0% -> 0%
where the time goes in v4:
time: 42 us; the launch traced here: 41.8 us
  waiting for transfers between devices  13.1 us (31%)
  starting transfers between devices  12.1 us (29%)
  other arithmetic  11.4 us (27%)
  local copies, waits for them, and re-layouts  2.91 us (7%)
  matrix products  1.93 us (5%)
    ppermute x7, waiting for transfers between devices, exchange(): return lax.ppermute(value, axis, [(i, i ^ mask) for i in range(count)])  13.1 us
    ppermute x7, starting transfers between devices, exchange(): return lax.ppermute(value, axis, [(i, i ^ mask) for i in range(count)])  11.4 us
    convert_element_type x3, other arithmetic, kernel_table(): cosine = (scaled * jnp.cos(phase)).astype(jnp.bfloat16)  9.04 us
    dot_general x4, matrix products, block_product(): return jnp.dot(flat, kernel, preferred_element_type=jnp.float32)  1.29 us
    convert_element_type x1, other arithmetic, local(): section_half = section_field.astype(jnp.bfloat16)  0.99 us
    reshape x2, local copies, waits for them, and re-layouts, local(): coded = positions.reshape(2, rows_here // halo_width, halo_width)  0.87 us
  transfers between devices with their start and end apart: 8, of which 5 were waited for; matrix products, arithmetic and copies ran while one was open for 31% of the time, Pallas kernels for 0%

profile of v4, /device:TPU:0, one launch (start us, length us, event | category | flops | bytes accessed | tf_op | source)
XLA Modules:
  0.0 41.8 jit_solution(13197307548411626392)
XLA Ops:
  0.0 0.8 %slice_bitcast_fusion.9 = (s32[64]{0:T(128)S(1)}, s32[64]{0:T(128)S(1)}) fusion(s32[2,64]{1,0:T(2,128)} %param.15), kind=kLoop, calls=%fused_computation.94 | loop fusion | bytes 1024 | tf_op jit(solution)/shard_map/squeeze | solution.py:60
  0.8 1.0 %fusion.38 = (bf16[2,128,128]{2,1,0:T(8,128)(2,1)S(1)}, f32[2,128,128]{2,1,0:T(8,128)S(1)}) fusion(f32[2,128,128]{2,1,0:T(8,128)} %param.8, f32[2,128,128]{2,1,0:T(8,128)} %param.9), kind=kLoop, calls=%fused_computation.101 | loop fusion | flops 98304 | bytes 458752 | tf_op jit(solution)/shard_map/convert_element_type | solution.py:55
  1.8 0.3 fusion.21
  2.1 0.7 %collective-permute-start.7 = (f32[2,128,64]{1,2,0:T(8,128)S(1)}, f32[2,128,64]{1,2,0:T(8,128)S(1)}, u32[]{:S(2)}, u32[]{:S(2)}) collective-permute-start(f32[2,128,64]{1,2,0:T(8,128)S(1)} %get-tuple-element.14), channel_id=1, source_target_pairs={{1,2},{3,4},{5,6},{7,8},{9,10},{11,12},{13,14},{15,16},{17,18},{19... | collective-permute-start | bytes 196616 | tf_op jit(solution)/shard_map/ppermute | solution.py:75
  2.8 0.8 %reshape.155 = f32[2,2,64]{2,1,0:T(2,128)S(1)} reshape(f32[2,128]{1,0:T(2,128)} %param.10) | data formatting | bytes 2048 | tf_op jit(solution)/shard_map/reshape | solution.py:77
  3.6 0.1 copy.44
  3.7 4.4 %collective-permute-start = (f32[2,130,64]{1,2,0:T(8,128)S(1)}, f32[2,130,64]{1,2,0:T(8,128)S(1)}, u32[]{:S(2)}, u32[]{:S(2)}) collective-permute-start(f32[2,130,64]{1,2,0:T(8,128)S(1)} %pad_maximum_fusion.3), channel_id=1, source_target_pairs={{0,1},{1,0},{2,3},{3,2},{4,5},{5,4},{6,7},{7,6},{8,9},{9,8},{10,11... | collective-permute-start | bytes 199688 | tf_op jit(solution)/shard_map/ppermute | solution.py:44
  8.2 2.9 %collective-permute-start.2 = (bf16[2,131,128]{2,1,0:T(8,128)(2,1)S(1)}, bf16[2,131,128]{2,1,0:T(8,128)(2,1)S(1)}, u32[]{:S(2)}, u32[]{:S(2)}) collective-permute-start(bf16[2,131,128]{2,1,0:T(8,128)(2,1)S(1)} %pad_maximum_fusion.5), channel_id=1, source_target_pairs={{0,16},{4,20},{8,24},{12,28},{16,0},{20,4},{24,8},{28,12},{1,17},{... | collective-permute-start | bytes 201224 | tf_op jit(solution)/shard_map/ppermute | solution.py:44
  11.3 1.3 %collective-permute-start.1 = (f32[2,256]{1,0:T(2,128)S(1)}, f32[2,256]{1,0:T(2,128)S(1)}, u32[]{:S(2)}, u32[]{:S(2)}) collective-permute-start(f32[2,256]{1,0:T(2,128)S(1)} %maximum_select_fusion.1), channel_id=1, source_target_pairs={{0,2},{1,3},{2,0},{3,1},{4,6},{5,7},{6,4},{7,5},{8,10},{9,11},{10,... | collective-permute-start | bytes 6152 | tf_op jit(solution)/shard_map/ppermute | solution.py:44
  12.6 2.7 %collective-permute-done.2 = bf16[2,131,128]{2,1,0:T(8,128)(2,1)S(1)} collective-permute-done((bf16[2,131,128]{2,1,0:T(8,128)(2,1)S(1)}, bf16[2,131,128]{2,1,0:T(8,128)(2,1)S(1)}, u32[]{:S(2)}, u32[]{:S(2)}) %collective-permute-start.2) | collective-permute-done | bytes 67104 | tf_op jit(solution)/shard_map/ppermute | solution.py:44
  15.4 0.8 %collective-permute-start.3 = (bf16[2,131,256]{2,1,0:T(8,128)(2,1)S(1)}, bf16[2,131,256]{2,1,0:T(8,128)(2,1)S(1)}, u32[]{:S(2)}, u32[]{:S(2)}) collective-permute-start(bf16[2,131,256]{2,1,0:T(8,128)(2,1)S(1)} %pad_maximum_fusion.2), channel_id=1, source_target_pairs={{0,8},{4,12},{8,0},{12,4},{16,24},{20,28},{24,16},{28,20},{1,9},{5... | collective-permute-start | bytes 402440 | tf_op jit(solution)/shard_map/ppermute | solution.py:44
  16.2 2.2 %multiply_convert_fusion.5 = (bf16[128,512]{1,0:T(8,128)(2,1)S(1)}, bf16[128,512]{1,0:T(8,128)(2,1)S(1)}, bf16[128,512]{1,0:T(8,128)(2,1)S(1)}, bf16[128,512]{1,0:T(8,128)(2,1)S(1)}) fusion(f32[128]{0:T(128)S(1)} %get-tuple-element.32, f32[128]{0:T(128)S(1)} %get-tuple-element.31, f32[512]{0:T(512)S(1)} %bitcast.81, f32[512]{0:T(512)S(1)} %bitcast.78, ...), kind=kLoop, calls=%fused_computation.35 | loop fusion | flops 1310720 | bytes 530432 | tf_op jit(solution)/shard_map/convert_element_type | solution.py:31
  18.5 0.3 fusion.8
  18.7 0.3 convolution_add_fusion.1
  19.0 1.4 %collective-permute-done.3 = bf16[2,131,256]{2,1,0:T(8,128)(2,1)S(1)} collective-permute-done((bf16[2,131,256]{2,1,0:T(8,128)(2,1)S(1)}, bf16[2,131,256]{2,1,0:T(8,128)(2,1)S(1)}, u32[]{:S(2)}, u32[]{:S(2)}) %collective-permute-start.3) | collective-permute-done | bytes 134176 | tf_op jit(solution)/shard_map/ppermute | solution.py:44
  20.5 1.2 %collective-permute-start.4 = (bf16[2,131,512]{2,1,0:T(8,128)(2,1)S(1)}, bf16[2,131,512]{2,1,0:T(8,128)(2,1)S(1)}, u32[]{:S(2)}, u32[]{:S(2)}) collective-permute-start(bf16[2,131,512]{2,1,0:T(8,128)(2,1)S(1)} %pad_maximum_fusion), channel_id=1, source_target_pairs={{0,4},{4,0},{8,12},{12,8},{16,20},{20,16},{24,28},{28,24},{1,5},{5... | collective-permute-start | bytes 804872 | tf_op jit(solution)/shard_map/ppermute | solution.py:44
  21.7 2.4 %multiply_convert_fusion.3 = (bf16[256,512]{1,0:T(8,128)(2,1)S(1)}, bf16[256,512]{1,0:T(8,128)(2,1)S(1)}) fusion(f32[256]{0:T(256)S(1)} %bitcast.87, f32[512]{0:T(512)S(1)} %bitcast.82, f32[256]{0:T(256)S(1)} %bitcast.86, f32[512]{0:T(512)S(1)} %bitcast.79), kind=kLoop, calls=%fused_computation.16 | loop fusion | flops 1310720 | bytes 530432 | tf_op jit(solution)/shard_map/convert_element_type | solution.py:31
  24.1 3.4 %collective-permute-done.4 = bf16[2,131,512]{2,1,0:T(8,128)(2,1)S(1)} collective-permute-done((bf16[2,131,512]{2,1,0:T(8,128)(2,1)S(1)}, bf16[2,131,512]{2,1,0:T(8,128)(2,1)S(1)}, u32[]{:S(2)}, u32[]{:S(2)}) %collective-permute-start.4) | collective-permute-done | bytes 268320 | tf_op jit(solution)/shard_map/ppermute | solution.py:44
  27.5 4.4 %multiply_convert_fusion.1 = (bf16[512,512]{1,0:T(8,128)(2,1)S(1)}, bf16[512,512]{1,0:T(8,128)(2,1)S(1)}) fusion(f32[512]{0:T(512)S(1)} %bitcast.85, f32[512]{0:T(512)S(1)} %bitcast.83, f32[512]{0:T(512)S(1)} %bitcast.84, f32[512]{0:T(512)S(1)} %bitcast.80), kind=kLoop, calls=%fused_computation.8 | loop fusion | flops 2621440 | bytes 1056768 | tf_op jit(solution)/shard_map/convert_element_type | solution.py:31
  32.0 0.4 %fusion.1 = f32[256,1024]{1,0:T(8,128)S(1)} fusion(bf16[256,512]{1,0:T(8,128)(2,1)S(1)} %bitcast.77, bf16[512,512]{1,0:T(8,128)(2,1)S(1)} %get-tuple-element.16, bf16[512,512]{1,0:T(8,128)(2,1)S(1)} %get-tuple-element.15), kind=kOutput, calls=%fused_computation.3 | convolution fusion | flops 270532608 | bytes 2359296 | tf_op jit(solution)/shard_map/dot_general | solution.py:39
  32.4 0.5 %slice-done = bf16[2,128,256]{2,1,0:T(8,128)(2,1)S(1)} async-done(((bf16[2,131,256]{2,1,0:T(8,128)(2,1)}), bf16[2,128,256]{2,1,0:T(8,128)(2,1)S(1)}, s32[]{:S(2)}) %slice-start) | async-done | bytes 131096 | tf_op jit(solution)/shard_map/slice | solution.py:110
  32.9 0.3 fusion
  33.3 0.2 stack.26
  33.5 0.2 stack.27
  33.8 0.1 copy.53
  33.9 0.1 copy.52
  34.0 0.1 pad_maximum_fusion.1
  34.2 1.2 %collective-permute-done.5 = f32[2,128,2,128]{3,1,0,2:T(8,128)S(1)} collective-permute-done((f32[2,128,2,128]{3,1,0,2:T(8,128)S(1)}, f32[2,128,2,128]{3,1,0,2:T(8,128)S(1)}, u32[]{:S(2)}, u32[]{:S(2)}) %collective-permute-start.5) | collective-permute-done | bytes 262176 | tf_op jit(solution)/shard_map/ppermute | solution.py:44
  35.4 0.8 %collective-permute-start.6 = (f32[2,128,1,128]{3,1,2,0:T(8,128)S(1)}, f32[2,128,1,128]{3,1,2,0:T(8,128)S(1)}, u32[]{:S(2)}, u32[]{:S(2)}) collective-permute-start(f32[2,128,1,128]{3,1,2,0:T(8,128)S(1)} %select_bitcast_fusion.1), channel_id=1, source_target_pairs={{0,2},{1,3},{2,0},{3,1},{4,6},{5,7},{6,4},{7,5},{8,10},{9,11},{10,... | collective-permute-start | bytes 393224 | tf_op jit(solution)/shard_map/ppermute | solution.py:44
  36.2 0.4 fusion.42
  36.6 4.4 %collective-permute-done.6 = f32[2,128,1,128]{3,1,2,0:T(8,128)S(1)} collective-permute-done((f32[2,128,1,128]{3,1,2,0:T(8,128)S(1)}, f32[2,128,1,128]{3,1,2,0:T(8,128)S(1)}, u32[]{:S(2)}, u32[]{:S(2)}) %collective-permute-start.6) | collective-permute-done | bytes 131104 | tf_op jit(solution)/shard_map/ppermute | solution.py:44
  41.1 0.7 %pad_maximum_fusion.4 = f32[2,128,128]{2,1,0:T(8,128)} fusion(f32[1,128,128]{2,1,0:T(8,128)S(1)} %get-tuple-element.10, f32[1,128,128]{2,1,0:T(8,128)S(1)} %get-tuple-element.9), kind=kLoop, calls=%fused_computation.42 | loop fusion | flops 32768 | bytes 262144 | tf_op jit(solution)/shard_map/stack | solution.py:152
  (52 shorter events, 0.9 us)
Async XLA Ops:
  0.0 8.1 %copy-start.1 = (f32[2,128]{1,0:T(2,128)S(1)}, f32[2,128]{1,0:T(2,128)}, u32[]{:S(2)}) copy-start(f32[2,128]{1,0:T(2,128)} %param.10) | copy-start | bytes 3076
  0.0 11.0 %copy-start.2 = (f32[6,128]{1,0:T(8,128)S(1)}, f32[6,128]{1,0:T(8,128)}, u32[]{:S(2)}) copy-start(f32[6,128]{1,0:T(8,128)} %param.13) | copy-start | bytes 9220
  0.0 11.0 %copy-start.3 = (s32[6,128]{1,0:T(8,128)S(1)}, s32[6,128]{1,0:T(8,128)}, u32[]{:S(2)}) copy-start(s32[6,128]{1,0:T(8,128)} %param.14) | copy-start | bytes 9220
  2.1 31.7 %collective-permute-start.7 = (f32[2,128,64]{1,2,0:T(8,128)S(1)}, f32[2,128,64]{1,2,0:T(8,128)S(1)}, u32[]{:S(2)}, u32[]{:S(2)}) collective-permute-start(f32[2,128,64]{1,2,0:T(8,128)S(1)} %get-tuple-element.14), channel_id=1, source_target_pairs={{1,2},{3,4},{5,6},{7,8},{9,10},{11,12},{13,14},{15,16},{17,18},{19... | collective-permute-start | bytes 196616 | tf_op jit(solution)/shard_map/ppermute | solution.py:75
  3.7 7.4 %collective-permute-start = (f32[2,130,64]{1,2,0:T(8,128)S(1)}, f32[2,130,64]{1,2,0:T(8,128)S(1)}, u32[]{:S(2)}, u32[]{:S(2)}) collective-permute-start(f32[2,130,64]{1,2,0:T(8,128)S(1)} %pad_maximum_fusion.3), channel_id=1, source_target_pairs={{0,1},{1,0},{2,3},{3,2},{4,5},{5,4},{6,7},{7,6},{8,9},{9,8},{10,11... | collective-permute-start | bytes 199688 | tf_op jit(solution)/shard_map/ppermute | solution.py:44
  8.2 7.2 %collective-permute-start.2 = (bf16[2,131,128]{2,1,0:T(8,128)(2,1)S(1)}, bf16[2,131,128]{2,1,0:T(8,128)(2,1)S(1)}, u32[]{:S(2)}, u32[]{:S(2)}) collective-permute-start(bf16[2,131,128]{2,1,0:T(8,128)(2,1)S(1)} %pad_maximum_fusion.5), channel_id=1, source_target_pairs={{0,16},{4,20},{8,24},{12,28},{16,0},{20,4},{24,8},{28,12},{1,17},{... | collective-permute-start | bytes 201224 | tf_op jit(solution)/shard_map/ppermute | solution.py:44
  11.3 4.9 %collective-permute-start.1 = (f32[2,256]{1,0:T(2,128)S(1)}, f32[2,256]{1,0:T(2,128)S(1)}, u32[]{:S(2)}, u32[]{:S(2)}) collective-permute-start(f32[2,256]{1,0:T(2,128)S(1)} %maximum_select_fusion.1), channel_id=1, source_target_pairs={{0,2},{1,3},{2,0},{3,1},{4,6},{5,7},{6,4},{7,5},{8,10},{9,11},{10,... | collective-permute-start | bytes 6152 | tf_op jit(solution)/shard_map/ppermute | solution.py:44
  15.4 5.1 %collective-permute-start.3 = (bf16[2,131,256]{2,1,0:T(8,128)(2,1)S(1)}, bf16[2,131,256]{2,1,0:T(8,128)(2,1)S(1)}, u32[]{:S(2)}, u32[]{:S(2)}) collective-permute-start(bf16[2,131,256]{2,1,0:T(8,128)(2,1)S(1)} %pad_maximum_fusion.2), channel_id=1, source_target_pairs={{0,8},{4,12},{8,0},{12,4},{16,24},{20,28},{24,16},{28,20},{1,9},{5... | collective-permute-start | bytes 402440 | tf_op jit(solution)/shard_map/ppermute | solution.py:44
  20.5 11.5 %copy-start = (bf16[2,131,256]{2,1,0:T(8,128)(2,1)}, bf16[2,131,256]{2,1,0:T(8,128)(2,1)S(1)}, u32[]{:S(2)}) copy-start(bf16[2,131,256]{2,1,0:T(8,128)(2,1)S(1)} %collective-permute-done.3) | copy-start | bytes 402436
  20.5 7.0 %collective-permute-start.4 = (bf16[2,131,512]{2,1,0:T(8,128)(2,1)S(1)}, bf16[2,131,512]{2,1,0:T(8,128)(2,1)S(1)}, u32[]{:S(2)}, u32[]{:S(2)}) collective-permute-start(bf16[2,131,512]{2,1,0:T(8,128)(2,1)S(1)} %pad_maximum_fusion), channel_id=1, source_target_pairs={{0,4},{4,0},{8,12},{12,8},{16,20},{20,16},{24,28},{28,24},{1,5},{5... | collective-permute-start | bytes 804872 | tf_op jit(solution)/shard_map/ppermute | solution.py:44
  32.0 0.9 %slice-start = ((bf16[2,131,256]{2,1,0:T(8,128)(2,1)}), bf16[2,128,256]{2,1,0:T(8,128)(2,1)S(1)}, s32[]{:S(2)}) async-start(bf16[2,131,256]{2,1,0:T(8,128)(2,1)} %copy-done), calls=%async_computation | async-start | bytes 262144 | tf_op jit(solution)/shard_map/slice | solution.py:110
  33.7 1.6 %collective-permute-start.5 = (f32[2,128,2,128]{3,1,0,2:T(8,128)S(1)}, f32[2,128,2,128]{3,1,0,2:T(8,128)S(1)}, u32[]{:S(2)}, u32[]{:S(2)}) collective-permute-start(f32[2,128,2,128]{3,1,0,2:T(8,128)S(1)} %select_bitcast_fusion), channel_id=1, source_target_pairs={{0,1},{1,0},{2,3},{3,2},{4,5},{5,4},{6,7},{7,6},{8,9},{9,8},{10,11... | collective-permute-start | bytes 786440 | tf_op jit(solution)/shard_map/ppermute | solution.py:44
  34.2 6.9 %copy-start.4 = (f32[128]{0:T(128)S(1)}, f32[128]{0:T(128)}, u32[]{:S(2)}) copy-start(f32[128]{0:T(128)} %param.12) | copy-start | bytes 1540
  34.2 6.9 %copy-start.5 = (f32[128]{0:T(128)S(1)}, f32[128]{0:T(128)}, u32[]{:S(2)}) copy-start(f32[128]{0:T(128)} %param.11) | copy-start | bytes 1540
  35.4 5.6 %collective-permute-start.6 = (f32[2,128,1,128]{3,1,2,0:T(8,128)S(1)}, f32[2,128,1,128]{3,1,2,0:T(8,128)S(1)}, u32[]{:S(2)}, u32[]{:S(2)}) collective-permute-start(f32[2,128,1,128]{3,1,2,0:T(8,128)S(1)} %select_bitcast_fusion.1), channel_id=1, source_target_pairs={{0,2},{1,3},{2,0},{3,1},{4,6},{5,7},{6,4},{7,5},{8,10},{9,11},{10,... | collective-permute-start | bytes 393224 | tf_op jit(solution)/shard_map/ppermute | solution.py:44

commit v5 on v4

--- a/solution.py
+++ b/solution.py
@@ -78,20 +78,14 @@
     first = exchange(jnp.concatenate([paired, coded], axis=1), "grp", 1)
     from_paired = first[:, :members]
     other = first[:, members:].reshape(2, rows_here)
-    targets = jnp.where(
-        odd,
-        jnp.concatenate([other, positions], axis=1),
-        jnp.concatenate([positions, other], axis=1),
-    )
+    targets = jnp.stack([positions, other], axis=1).reshape(2, -1)
     mask = 2
     while mask < group:
         other = exchange(targets, "grp", mask)
-        upper = (where_in_group & mask) != 0
-        targets = jnp.where(
-            upper,
-            jnp.concatenate([other, targets], axis=1),
-            jnp.concatenate([targets, other], axis=1),
-        )
+        count = targets.shape[1] // rows_here
+        targets = jnp.stack(
+            [targets.reshape(2, count, rows_here), other.reshape(2, count, rows_here)], axis=2
+        ).reshape(2, -1)
         mask *= 2
     width = targets.shape[1]
     from_prev = jnp.where(odd, from_paired, from_crossed)
@@ -117,15 +111,10 @@
         ]
     )
 
-    count = group
     mask = 1
     while mask < group:
-        split = partial.reshape(2, members, count // 2, 2, rows_here)
-        upper = (where_in_group & mask) != 0
-        keep = jnp.where(upper, split[:, :, :, 1], split[:, :, :, 0])
-        give = jnp.where(upper, split[:, :, :, 0], split[:, :, :, 1])
-        partial = (keep + exchange(give, "grp", mask)).reshape(2, members, -1)
-        count //= 2
+        half = partial.shape[2] // 2
+        partial = partial[:, :, :half] + exchange(partial[:, :, half:], "grp", mask)
         mask *= 2
     real_part = partial[0]
     imag_part = partial[1]

time: 42 us -> 41.6 us (level)
  transfers between devices with their start and end apart: 8 -> 8, of which waited for: 5 -> 5; matrix products, arithmetic and copies ran while one was open for 31% -> 30% of each run, Pallas kernels for 0% -> 0%
where the time goes in v5:
time: 41.6 us; the launch traced here: 41.3 us
  waiting for transfers between devices  13.1 us (31%)
  starting transfers between devices  12.1 us (29%)
  other arithmetic  11.3 us (27%)
  local copies, waits for them, and re-layouts  2.54 us (6%)
  matrix products  1.93 us (5%)
    ppermute x7, waiting for transfers between devices, exchange(): return lax.ppermute(value, axis, [(i, i ^ mask) for i in range(count)])  13.1 us
    ppermute x7, starting transfers between devices, exchange(): return lax.ppermute(value, axis, [(i, i ^ mask) for i in range(count)])  11.4 us
    convert_element_type x3, other arithmetic, kernel_table(): cosine = (scaled * jnp.cos(phase)).astype(jnp.bfloat16)  9.04 us
    dot_general x4, matrix products, block_product(): return jnp.dot(flat, kernel, preferred_element_type=jnp.float32)  1.28 us
    convert_element_type x1, other arithmetic, local(): section_half = section_field.astype(jnp.bfloat16)  0.99 us
    reshape x2, local copies, waits for them, and re-layouts, local(): coded = positions.reshape(2, rows_here // halo_width, halo_width)  0.87 us
  transfers between devices with their start and end apart: 8, of which 5 were waited for; matrix products, arithmetic and copies ran while one was open for 30% of the time, Pallas kernels for 0%

profile of v5, /device:TPU:0, one launch (start us, length us, event | category | flops | bytes accessed | tf_op | source)
XLA Modules:
  0.0 41.3 jit_solution(14830997546788015427)
XLA Ops:
  0.0 0.8 %slice_bitcast_fusion.7 = (s32[64]{0:T(128)S(1)}, s32[64]{0:T(128)S(1)}) fusion(s32[2,64]{1,0:T(2,128)} %param.15), kind=kLoop, calls=%fused_computation.98 | loop fusion | bytes 1024 | tf_op jit(solution)/shard_map/squeeze | solution.py:60
  0.8 1.0 %fusion.42 = (bf16[2,128,128]{2,1,0:T(8,128)(2,1)S(1)}, f32[2,128,128]{2,1,0:T(8,128)S(1)}) fusion(f32[2,128,128]{2,1,0:T(8,128)} %param.8, f32[2,128,128]{2,1,0:T(8,128)} %param.9), kind=kLoop, calls=%fused_computation.105 | loop fusion | flops 98304 | bytes 458752 | tf_op jit(solution)/shard_map/convert_element_type | solution.py:55
  1.8 0.3 fusion.22
  2.1 0.7 %collective-permute-start.7 = (f32[2,128,64]{1,2,0:T(8,128)S(1)}, f32[2,128,64]{1,2,0:T(8,128)S(1)}, u32[]{:S(2)}, u32[]{:S(2)}) collective-permute-start(f32[2,128,64]{1,2,0:T(8,128)S(1)} %get-tuple-element.14), channel_id=1, source_target_pairs={{1,2},{3,4},{5,6},{7,8},{9,10},{11,12},{13,14},{15,16},{17,18},{19... | collective-permute-start | bytes 196616 | tf_op jit(solution)/shard_map/ppermute | solution.py:75
  2.8 0.8 %reshape.100 = f32[2,2,64]{2,1,0:T(2,128)S(1)} reshape(f32[2,128]{1,0:T(2,128)} %param.10) | data formatting | bytes 2048 | tf_op jit(solution)/shard_map/reshape | solution.py:77
  3.6 0.1 copy.38
  3.7 4.4 %collective-permute-start = (f32[2,130,64]{1,2,0:T(8,128)S(1)}, f32[2,130,64]{1,2,0:T(8,128)S(1)}, u32[]{:S(2)}, u32[]{:S(2)}) collective-permute-start(f32[2,130,64]{1,2,0:T(8,128)S(1)} %pad_maximum_fusion.4), channel_id=1, source_target_pairs={{0,1},{1,0},{2,3},{3,2},{4,5},{5,4},{6,7},{7,6},{8,9},{9,8},{10,11... | collective-permute-start | bytes 199688 | tf_op jit(solution)/shard_map/ppermute | solution.py:44
  8.2 2.9 %collective-permute-start.2 = (bf16[2,131,128]{2,1,0:T(8,128)(2,1)S(1)}, bf16[2,131,128]{2,1,0:T(8,128)(2,1)S(1)}, u32[]{:S(2)}, u32[]{:S(2)}) collective-permute-start(bf16[2,131,128]{2,1,0:T(8,128)(2,1)S(1)} %pad_maximum_fusion.6), channel_id=1, source_target_pairs={{0,16},{4,20},{8,24},{12,28},{16,0},{20,4},{24,8},{28,12},{1,17},{... | collective-permute-start | bytes 201224 | tf_op jit(solution)/shard_map/ppermute | solution.py:44
  11.0 0.1 select_reduce_fusion
  11.2 0.1 stack_reshape.6
  11.3 1.3 %collective-permute-start.1 = (f32[2,256]{1,0:T(2,128)S(1)}, f32[2,256]{1,0:T(2,128)S(1)}, u32[]{:S(2)}, u32[]{:S(2)}) collective-permute-start(f32[2,256]{1,0:T(2,128)S(1)} %get-tuple-element.32), channel_id=1, source_target_pairs={{0,2},{1,3},{2,0},{3,1},{4,6},{5,7},{6,4},{7,5},{8,10},{9,11},{10,... | collective-permute-start | bytes 6152 | tf_op jit(solution)/shard_map/ppermute | solution.py:44
  12.6 2.7 %collective-permute-done.2 = bf16[2,131,128]{2,1,0:T(8,128)(2,1)S(1)} collective-permute-done((bf16[2,131,128]{2,1,0:T(8,128)(2,1)S(1)}, bf16[2,131,128]{2,1,0:T(8,128)(2,1)S(1)}, u32[]{:S(2)}, u32[]{:S(2)}) %collective-permute-start.2) | collective-permute-done | bytes 67104 | tf_op jit(solution)/shard_map/ppermute | solution.py:44
  15.4 0.8 %collective-permute-start.3 = (bf16[2,131,256]{2,1,0:T(8,128)(2,1)S(1)}, bf16[2,131,256]{2,1,0:T(8,128)(2,1)S(1)}, u32[]{:S(2)}, u32[]{:S(2)}) collective-permute-start(bf16[2,131,256]{2,1,0:T(8,128)(2,1)S(1)} %pad_maximum_fusion.3), channel_id=1, source_target_pairs={{0,8},{4,12},{8,0},{12,4},{16,24},{20,28},{24,16},{28,20},{1,9},{5... | collective-permute-start | bytes 402440 | tf_op jit(solution)/shard_map/ppermute | solution.py:44
  16.2 2.2 %multiply_convert_fusion.5 = (bf16[128,512]{1,0:T(8,128)(2,1)S(1)}, bf16[128,512]{1,0:T(8,128)(2,1)S(1)}, bf16[128,512]{1,0:T(8,128)(2,1)S(1)}, bf16[128,512]{1,0:T(8,128)(2,1)S(1)}) fusion(f32[128]{0:T(128)S(1)} %get-tuple-element.34, f32[128]{0:T(128)S(1)} %get-tuple-element.33, f32[512]{0:T(512)S(1)} %bitcast.62, f32[512]{0:T(512)S(1)} %bitcast.65, ...), kind=kLoop, calls=%fused_computation.37 | loop fusion | flops 1310720 | bytes 530432 | tf_op jit(solution)/shard_map/convert_element_type | solution.py:31
  18.5 0.3 fusion.12
  18.7 0.3 convolution_add_fusion.1
  19.0 1.4 %collective-permute-done.3 = bf16[2,131,256]{2,1,0:T(8,128)(2,1)S(1)} collective-permute-done((bf16[2,131,256]{2,1,0:T(8,128)(2,1)S(1)}, bf16[2,131,256]{2,1,0:T(8,128)(2,1)S(1)}, u32[]{:S(2)}, u32[]{:S(2)}) %collective-permute-start.3) | collective-permute-done | bytes 134176 | tf_op jit(solution)/shard_map/ppermute | solution.py:44
  20.5 1.2 %collective-permute-start.4 = (bf16[2,131,512]{2,1,0:T(8,128)(2,1)S(1)}, bf16[2,131,512]{2,1,0:T(8,128)(2,1)S(1)}, u32[]{:S(2)}, u32[]{:S(2)}) collective-permute-start(bf16[2,131,512]{2,1,0:T(8,128)(2,1)S(1)} %pad_maximum_fusion), channel_id=1, source_target_pairs={{0,4},{4,0},{8,12},{12,8},{16,20},{20,16},{24,28},{28,24},{1,5},{5... | collective-permute-start | bytes 804872 | tf_op jit(solution)/shard_map/ppermute | solution.py:44
  21.7 2.4 %multiply_convert_fusion.3 = (bf16[256,512]{1,0:T(8,128)(2,1)S(1)}, bf16[256,512]{1,0:T(8,128)(2,1)S(1)}) fusion(f32[256]{0:T(256)S(1)} %bitcast.72, f32[512]{0:T(512)S(1)} %bitcast.63, f32[256]{0:T(256)S(1)} %bitcast.71, f32[512]{0:T(512)S(1)} %bitcast.66), kind=kLoop, calls=%fused_computation.18 | loop fusion | flops 1310720 | bytes 530432 | tf_op jit(solution)/shard_map/convert_element_type | solution.py:31
  24.1 3.4 %collective-permute-done.4 = bf16[2,131,512]{2,1,0:T(8,128)(2,1)S(1)} collective-permute-done((bf16[2,131,512]{2,1,0:T(8,128)(2,1)S(1)}, bf16[2,131,512]{2,1,0:T(8,128)(2,1)S(1)}, u32[]{:S(2)}, u32[]{:S(2)}) %collective-permute-start.4) | collective-permute-done | bytes 268320 | tf_op jit(solution)/shard_map/ppermute | solution.py:44
  27.5 4.4 %multiply_convert_fusion.1 = (bf16[512,512]{1,0:T(8,128)(2,1)S(1)}, bf16[512,512]{1,0:T(8,128)(2,1)S(1)}) fusion(f32[512]{0:T(512)S(1)} %bitcast.70, f32[512]{0:T(512)S(1)} %bitcast.64, f32[512]{0:T(512)S(1)} %bitcast.69, f32[512]{0:T(512)S(1)} %bitcast.67), kind=kLoop, calls=%fused_computation.8 | loop fusion | flops 2621440 | bytes 1056768 | tf_op jit(solution)/shard_map/convert_element_type | solution.py:31
  32.0 0.4 %fusion.1 = f32[256,1024]{1,0:T(8,128)S(1)} fusion(bf16[256,512]{1,0:T(8,128)(2,1)S(1)} %bitcast.61, bf16[512,512]{1,0:T(8,128)(2,1)S(1)} %get-tuple-element.16, bf16[512,512]{1,0:T(8,128)(2,1)S(1)} %get-tuple-element.15), kind=kOutput, calls=%fused_computation.3 | convolution fusion | flops 270532608 | bytes 2359296 | tf_op jit(solution)/shard_map/dot_general | solution.py:39
  32.4 0.5 %slice-done = bf16[2,128,256]{2,1,0:T(8,128)(2,1)S(1)} async-done(((bf16[2,131,256]{2,1,0:T(8,128)(2,1)}), bf16[2,128,256]{2,1,0:T(8,128)(2,1)S(1)}, s32[]{:S(2)}) %slice-start) | async-done | bytes 131096 | tf_op jit(solution)/shard_map/slice | solution.py:104
  32.9 0.3 fusion
  33.4 0.1 copy.46
  33.5 0.1 copy.45
  33.6 0.1 pad_maximum_fusion.2
  33.8 1.2 %collective-permute-done.5 = f32[2,128,256]{2,1,0:T(8,128)S(1)} collective-permute-done((f32[2,128,256]{2,1,0:T(8,128)S(1)}, f32[2,128,256]{2,1,0:T(8,128)S(1)}, u32[]{:S(2)}, u32[]{:S(2)}) %collective-permute-start.5) | collective-permute-done | bytes 262176 | tf_op jit(solution)/shard_map/ppermute | solution.py:44
  35.0 0.8 %collective-permute-start.6 = (f32[2,128,128]{2,1,0:T(8,128)S(1)}, f32[2,128,128]{2,1,0:T(8,128)S(1)}, u32[]{:S(2)}, u32[]{:S(2)}) collective-permute-start(f32[2,128,128]{2,1,0:T(8,128)S(1)} %slice.216), channel_id=1, source_target_pairs={{0,2},{1,3},{2,0},{3,1},{4,6},{5,7},{6,4},{7,5},{8,10},{9,11},{10,... | collective-permute-start | bytes 393224 | tf_op jit(solution)/shard_map/ppermute | solution.py:44
  35.8 0.4 fusion.45
  36.1 4.4 %collective-permute-done.6 = f32[2,128,128]{2,1,0:T(8,128)S(1)} collective-permute-done((f32[2,128,128]{2,1,0:T(8,128)S(1)}, f32[2,128,128]{2,1,0:T(8,128)S(1)}, u32[]{:S(2)}, u32[]{:S(2)}) %collective-permute-start.6) | collective-permute-done | bytes 131104 | tf_op jit(solution)/shard_map/ppermute | solution.py:44
  40.7 0.7 %pad_maximum_fusion.5 = f32[2,128,128]{2,1,0:T(8,128)} fusion(f32[1,128,128]{2,1,0:T(8,128)S(1)} %get-tuple-element.10, f32[1,128,128]{2,1,0:T(8,128)S(1)} %get-tuple-element.9), kind=kLoop, calls=%fused_computation.45 | loop fusion | flops 32768 | bytes 262144 | tf_op jit(solution)/shard_map/stack | solution.py:141
  (49 shorter events, 0.7 us)
Async XLA Ops:
  0.0 8.1 %copy-start.1 = (f32[2,128]{1,0:T(2,128)S(1)}, f32[2,128]{1,0:T(2,128)}, u32[]{:S(2)}) copy-start(f32[2,128]{1,0:T(2,128)} %param.10) | copy-start | bytes 3076
  0.0 11.0 %copy-start.2 = (f32[6,128]{1,0:T(8,128)S(1)}, f32[6,128]{1,0:T(8,128)}, u32[]{:S(2)}) copy-start(f32[6,128]{1,0:T(8,128)} %param.13) | copy-start | bytes 9220
  0.0 11.0 %copy-start.3 = (s32[6,128]{1,0:T(8,128)S(1)}, s32[6,128]{1,0:T(8,128)}, u32[]{:S(2)}) copy-start(s32[6,128]{1,0:T(8,128)} %param.14) | copy-start | bytes 9220
  2.1 31.3 %collective-permute-start.7 = (f32[2,128,64]{1,2,0:T(8,128)S(1)}, f32[2,128,64]{1,2,0:T(8,128)S(1)}, u32[]{:S(2)}, u32[]{:S(2)}) collective-permute-start(f32[2,128,64]{1,2,0:T(8,128)S(1)} %get-tuple-element.14), channel_id=1, source_target_pairs={{1,2},{3,4},{5,6},{7,8},{9,10},{11,12},{13,14},{15,16},{17,18},{19... | collective-permute-start | bytes 196616 | tf_op jit(solution)/shard_map/ppermute | solution.py:75
  3.7 7.4 %collective-permute-start = (f32[2,130,64]{1,2,0:T(8,128)S(1)}, f32[2,130,64]{1,2,0:T(8,128)S(1)}, u32[]{:S(2)}, u32[]{:S(2)}) collective-permute-start(f32[2,130,64]{1,2,0:T(8,128)S(1)} %pad_maximum_fusion.4), channel_id=1, source_target_pairs={{0,1},{1,0},{2,3},{3,2},{4,5},{5,4},{6,7},{7,6},{8,9},{9,8},{10,11... | collective-permute-start | bytes 199688 | tf_op jit(solution)/shard_map/ppermute | solution.py:44
  8.2 7.2 %collective-permute-start.2 = (bf16[2,131,128]{2,1,0:T(8,128)(2,1)S(1)}, bf16[2,131,128]{2,1,0:T(8,128)(2,1)S(1)}, u32[]{:S(2)}, u32[]{:S(2)}) collective-permute-start(bf16[2,131,128]{2,1,0:T(8,128)(2,1)S(1)} %pad_maximum_fusion.6), channel_id=1, source_target_pairs={{0,16},{4,20},{8,24},{12,28},{16,0},{20,4},{24,8},{28,12},{1,17},{... | collective-permute-start | bytes 201224 | tf_op jit(solution)/shard_map/ppermute | solution.py:44
  11.3 4.9 %collective-permute-start.1 = (f32[2,256]{1,0:T(2,128)S(1)}, f32[2,256]{1,0:T(2,128)S(1)}, u32[]{:S(2)}, u32[]{:S(2)}) collective-permute-start(f32[2,256]{1,0:T(2,128)S(1)} %get-tuple-element.32), channel_id=1, source_target_pairs={{0,2},{1,3},{2,0},{3,1},{4,6},{5,7},{6,4},{7,5},{8,10},{9,11},{10,... | collective-permute-start | bytes 6152 | tf_op jit(solution)/shard_map/ppermute | solution.py:44
  15.4 5.1 %collective-permute-start.3 = (bf16[2,131,256]{2,1,0:T(8,128)(2,1)S(1)}, bf16[2,131,256]{2,1,0:T(8,128)(2,1)S(1)}, u32[]{:S(2)}, u32[]{:S(2)}) collective-permute-start(bf16[2,131,256]{2,1,0:T(8,128)(2,1)S(1)} %pad_maximum_fusion.3), channel_id=1, source_target_pairs={{0,8},{4,12},{8,0},{12,4},{16,24},{20,28},{24,16},{28,20},{1,9},{5... | collective-permute-start | bytes 402440 | tf_op jit(solution)/shard_map/ppermute | solution.py:44
  20.5 11.5 %copy-start = (bf16[2,131,256]{2,1,0:T(8,128)(2,1)}, bf16[2,131,256]{2,1,0:T(8,128)(2,1)S(1)}, u32[]{:S(2)}) copy-start(bf16[2,131,256]{2,1,0:T(8,128)(2,1)S(1)} %collective-permute-done.3) | copy-start | bytes 402436
  20.5 7.0 %collective-permute-start.4 = (bf16[2,131,512]{2,1,0:T(8,128)(2,1)S(1)}, bf16[2,131,512]{2,1,0:T(8,128)(2,1)S(1)}, u32[]{:S(2)}, u32[]{:S(2)}) collective-permute-start(bf16[2,131,512]{2,1,0:T(8,128)(2,1)S(1)} %pad_maximum_fusion), channel_id=1, source_target_pairs={{0,4},{4,0},{8,12},{12,8},{16,20},{20,16},{24,28},{28,24},{1,5},{5... | collective-permute-start | bytes 804872 | tf_op jit(solution)/shard_map/ppermute | solution.py:44
  32.0 0.9 %slice-start = ((bf16[2,131,256]{2,1,0:T(8,128)(2,1)}), bf16[2,128,256]{2,1,0:T(8,128)(2,1)S(1)}, s32[]{:S(2)}) async-start(bf16[2,131,256]{2,1,0:T(8,128)(2,1)} %copy-done), calls=%async_computation | async-start | bytes 262144 | tf_op jit(solution)/shard_map/slice | solution.py:104
  33.3 1.6 %collective-permute-start.5 = (f32[2,128,256]{2,1,0:T(8,128)S(1)}, f32[2,128,256]{2,1,0:T(8,128)S(1)}, u32[]{:S(2)}, u32[]{:S(2)}) collective-permute-start(f32[2,128,256]{2,1,0:T(8,128)S(1)} %pad_maximum_fusion.1), channel_id=1, source_target_pairs={{0,1},{1,0},{2,3},{3,2},{4,5},{5,4},{6,7},{7,6},{8,9},{9,8},{10,11... | collective-permute-start | bytes 786440 | tf_op jit(solution)/shard_map/ppermute | solution.py:44
  33.7 6.9 %copy-start.4 = (f32[128]{0:T(128)S(1)}, f32[128]{0:T(128)}, u32[]{:S(2)}) copy-start(f32[128]{0:T(128)} %param.12) | copy-start | bytes 1540
  33.7 6.9 %copy-start.5 = (f32[128]{0:T(128)S(1)}, f32[128]{0:T(128)}, u32[]{:S(2)}) copy-start(f32[128]{0:T(128)} %param.11) | copy-start | bytes 1540
  35.0 5.6 %collective-permute-start.6 = (f32[2,128,128]{2,1,0:T(8,128)S(1)}, f32[2,128,128]{2,1,0:T(8,128)S(1)}, u32[]{:S(2)}, u32[]{:S(2)}) collective-permute-start(f32[2,128,128]{2,1,0:T(8,128)S(1)} %slice.216), channel_id=1, source_target_pairs={{0,2},{1,3},{2,0},{3,1},{4,6},{5,7},{6,4},{7,5},{8,10},{9,11},{10,... | collective-permute-start | bytes 393224 | tf_op jit(solution)/shard_map/ppermute | solution.py:44

commit v6 on v5

--- a/solution.py
+++ b/solution.py
@@ -94,16 +94,26 @@
     pieces = jnp.stack(bf16_pieces(positions), axis=1)
     payload = jnp.concatenate([section_half, pieces], axis=1)
     product = block_product(section_half, positions, targets, scaled)
-    gathered = payload
-    mask = blocks // 2
-    while mask >= 1:
-        received = exchange(gathered, "blk", mask)
+    def add_blocks(product, received):
         place = from_pieces(
             received[:, members], received[:, members + 1], received[:, members + 2]
         )
-        product = product + block_product(received[:, :members], place, targets, scaled)
+        return product + block_product(received[:, :members], place, targets, scaled)
+
+    masks = []
+    mask = blocks // 2
+    while mask >= 1:
+        masks.append(mask)
+        mask //= 2
+    last = masks[-2:] if len(masks) >= 2 else []
+    gathered = payload
+    for mask in masks[: len(masks) - len(last)]:
+        received = exchange(gathered, "blk", mask)
+        product = add_blocks(product, received)
         gathered = jnp.concatenate([gathered, received], axis=2)
-        mask //= 2
+    if last:
+        for mask in (last[0], last[1], last[0] ^ last[1]):
+            product = add_blocks(product, exchange(gathered, "blk", mask))
     partial = jnp.stack(
         [
             product[:members, :width] - product[members:, width:],

time: 41.6 us -> 39 us (0.938)
  waiting for transfers between devices: 13.1 us -> 9.35 us
  starting transfers between devices: 12.1 us -> 13.4 us
  local copies, waits for them, and re-layouts: 2.54 us -> 1.9 us
    ppermute x7 -> x8, waiting for transfers between devices: 13.1 us -> 9.34 us  [exchange(): return lax.ppermute(value, axis, [(i, i ^ mask) for i in range(count)])]
    ppermute x7 -> x8, starting transfers between devices: 11.4 us -> 12.8 us  [exchange(): return lax.ppermute(value, axis, [(i, i ^ mask) for i in range(count)])]
    squeeze x1, local copies, waits for them, and re-layouts: 0.76 us -> 0.01 us  [local(): listed = jnp.concatenate([send_list[1], send_list[0]])]
    unnamed x12 -> x14, local copies, waits for them, and re-layouts: 0.03 us -> 0.71 us
    reshape x2, local copies, waits for them, and re-layouts: 0.87 us -> 0.19 us  [local(): coded = positions.reshape(2, rows_here // halo_width, halo_width)]
    another operation x1, other arithmetic: 0.01 us -> 0.68 us  [local(): pieces = jnp.stack(bf16_pieces(positions), axis=1)]
    convert_element_type x3 -> x2, other arithmetic: 9.04 us -> 8.69 us  [kernel_table(): cosine = (scaled * jnp.cos(phase)).astype(jnp.bfloat16)]
    dot_general x4 -> x5, matrix products: 1.28 us -> 1.46 us  [block_product(): return jnp.dot(flat, kernel, preferred_element_type=jnp.float32)]
  transfers between devices with their start and end apart: 8 -> 9, of which waited for: 5 -> 6; matrix products, arithmetic and copies ran while one was open for 30% -> 31% of each run, Pallas kernels for 0% -> 0%
where the time goes in v6:
time: 39 us; the launch traced here: 38.8 us
  starting transfers between devices  13.4 us (34%)
  other arithmetic  11.6 us (30%)
  waiting for transfers between devices  9.35 us (24%)
  matrix products  2.1 us (5%)
  local copies, waits for them, and re-layouts  1.9 us (5%)
    ppermute x8, starting transfers between devices, exchange(): return lax.ppermute(value, axis, [(i, i ^ mask) for i in range(count)])  12.8 us
    ppermute x8, waiting for transfers between devices, exchange(): return lax.ppermute(value, axis, [(i, i ^ mask) for i in range(count)])  9.34 us
    convert_element_type x2, other arithmetic, kernel_table(): cosine = (scaled * jnp.cos(phase)).astype(jnp.bfloat16)  8.69 us
    dot_general x5, matrix products, block_product(): return jnp.dot(flat, kernel, preferred_element_type=jnp.float32)  1.46 us
    convert_element_type x1, other arithmetic, local(): section_half = section_field.astype(jnp.bfloat16)  0.99 us
  transfers between devices with their start and end apart: 9, of which 6 were waited for; matrix products, arithmetic and copies ran while one was open for 31% of the time, Pallas kernels for 0%

profile of v6, /device:TPU:0, one launch (start us, length us, event | category | flops | bytes accessed | tf_op | source)
XLA Modules:
  0.0 38.8 jit_solution(16661416579792821819)
XLA Ops:
  0.0 0.7 %fusion.42 = (bf16[2,1,128]{2,0,1:T(2,128)(2,1)S(1)}, bf16[2,1,128]{2,0,1:T(2,128)(2,1)S(1)}, bf16[2,1,128]{2,0,1:T(2,128)(2,1)S(1)}) fusion(f32[2,128]{1,0:T(2,128)} %param.10), kind=kLoop, calls=%fused_computation.103 | loop fusion | flops 1792 | bytes 2560 | tf_op jit(solution)/shard_map/stack | solution.py:94
  0.7 1.0 %fusion.50 = (bf16[2,128,128]{2,1,0:T(8,128)(2,1)S(1)}, f32[2,128,128]{2,1,0:T(8,128)S(1)}) fusion(f32[2,128,128]{2,1,0:T(8,128)} %param.8, f32[2,128,128]{2,1,0:T(8,128)} %param.9), kind=kLoop, calls=%fused_computation.118 | loop fusion | flops 98304 | bytes 458752 | tf_op jit(solution)/shard_map/convert_element_type | solution.py:55
  1.7 4.1 %collective-permute-start.2 = (bf16[2,131,128]{2,1,0:T(8,128)(2,1)S(1)}, bf16[2,131,128]{2,1,0:T(8,128)(2,1)S(1)}, u32[]{:S(2)}, u32[]{:S(2)}) collective-permute-start(bf16[2,131,128]{2,1,0:T(8,128)(2,1)S(1)} %pad_maximum_fusion.5), channel_id=1, source_target_pairs={{0,16},{4,20},{8,24},{12,28},{16,0},{20,4},{24,8},{28,12},{1,17},{... | collective-permute-start | bytes 201224 | tf_op jit(solution)/shard_map/ppermute | solution.py:44
  5.9 0.7 %copy-done.4 = s32[2,64]{1,0:T(2,128)S(1)} copy-done((s32[2,64]{1,0:T(2,128)S(1)}, s32[2,64]{1,0:T(2,128)}, u32[]{:S(2)}) %copy-start.4) | copy-done | bytes 536
  6.6 0.3 fusion.27
  6.9 0.7 %collective-permute-start.8 = (f32[2,128,64]{1,2,0:T(8,128)S(1)}, f32[2,128,64]{1,2,0:T(8,128)S(1)}, u32[]{:S(2)}, u32[]{:S(2)}) collective-permute-start(f32[2,128,64]{1,2,0:T(8,128)S(1)} %get-tuple-element.14), channel_id=1, source_target_pairs={{1,2},{3,4},{5,6},{7,8},{9,10},{11,12},{13,14},{15,16},{17,18},{19... | collective-permute-start | bytes 196616 | tf_op jit(solution)/shard_map/ppermute | solution.py:75
  7.7 0.1 copy.38
  7.8 2.9 %collective-permute-start = (f32[2,130,64]{1,2,0:T(8,128)S(1)}, f32[2,130,64]{1,2,0:T(8,128)S(1)}, u32[]{:S(2)}, u32[]{:S(2)}) collective-permute-start(f32[2,130,64]{1,2,0:T(8,128)S(1)} %pad_maximum_fusion.3), channel_id=1, source_target_pairs={{0,1},{1,0},{2,3},{3,2},{4,5},{5,4},{6,7},{7,6},{8,9},{9,8},{10,11... | collective-permute-start | bytes 199688 | tf_op jit(solution)/shard_map/ppermute | solution.py:44
  10.9 0.9 %collective-permute-done = f32[2,130,64]{1,2,0:T(8,128)S(1)} collective-permute-done((f32[2,130,64]{1,2,0:T(8,128)S(1)}, f32[2,130,64]{1,2,0:T(8,128)S(1)}, u32[]{:S(2)}, u32[]{:S(2)}) %collective-permute-start) | collective-permute-done | bytes 66592 | tf_op jit(solution)/shard_map/ppermute | solution.py:44
  11.8 0.1 stack_reshape.6
  11.9 1.5 %collective-permute-start.1 = (f32[2,256]{1,0:T(2,128)S(1)}, f32[2,256]{1,0:T(2,128)S(1)}, u32[]{:S(2)}, u32[]{:S(2)}) collective-permute-start(f32[2,256]{1,0:T(2,128)S(1)} %get-tuple-element.38), channel_id=1, source_target_pairs={{0,2},{1,3},{2,0},{3,1},{4,6},{5,7},{6,4},{7,5},{8,10},{9,11},{10,... | collective-permute-start | bytes 6152 | tf_op jit(solution)/shard_map/ppermute | solution.py:44
  13.5 1.4 %collective-permute-start.5 = (bf16[2,131,256]{2,1,0:T(8,128)(2,1)S(1)}, bf16[2,131,256]{2,1,0:T(8,128)(2,1)S(1)}, u32[]{:S(2)}, u32[]{:S(2)}) collective-permute-start(bf16[2,131,256]{2,1,0:T(8,128)(2,1)S(1)} %pad_maximum_fusion.2), channel_id=1, source_target_pairs={{0,12},{4,8},{8,4},{12,0},{16,28},{20,24},{24,20},{28,16},{1,13},{... | collective-permute-start | bytes 402440 | tf_op jit(solution)/shard_map/ppermute | solution.py:44
  14.8 1.7 %collective-permute-start.4 = (bf16[2,131,256]{2,1,0:T(8,128)(2,1)S(1)}, bf16[2,131,256]{2,1,0:T(8,128)(2,1)S(1)}, u32[]{:S(2)}, u32[]{:S(2)}) collective-permute-start(bf16[2,131,256]{2,1,0:T(8,128)(2,1)S(1)} %pad_maximum_fusion.2), channel_id=1, source_target_pairs={{0,4},{4,0},{8,12},{12,8},{16,20},{20,16},{24,28},{28,24},{1,5},{5... | collective-permute-start | bytes 402440 | tf_op jit(solution)/shard_map/ppermute | solution.py:44
  16.6 0.4 %collective-permute-start.3 = (bf16[2,131,256]{2,1,0:T(8,128)(2,1)S(1)}, bf16[2,131,256]{2,1,0:T(8,128)(2,1)S(1)}, u32[]{:S(2)}, u32[]{:S(2)}) collective-permute-start(bf16[2,131,256]{2,1,0:T(8,128)(2,1)S(1)} %pad_maximum_fusion.2), channel_id=1, source_target_pairs={{0,8},{4,12},{8,0},{12,4},{16,24},{20,28},{24,16},{28,20},{1,9},{5... | collective-permute-start | bytes 402440 | tf_op jit(solution)/shard_map/ppermute | solution.py:44
  17.1 2.2 %multiply_convert_fusion.7 = (bf16[128,512]{1,0:T(8,128)(2,1)S(1)}, bf16[128,512]{1,0:T(8,128)(2,1)S(1)}, bf16[128,512]{1,0:T(8,128)(2,1)S(1)}, bf16[128,512]{1,0:T(8,128)(2,1)S(1)}) fusion(f32[128]{0:T(128)S(1)} %get-tuple-element.42, f32[128]{0:T(128)S(1)} %get-tuple-element.41, f32[512]{0:T(512)S(1)} %bitcast.69, f32[512]{0:T(512)S(1)} %bitcast.67, ...), kind=kLoop, calls=%fused_computation.44 | loop fusion | flops 1310720 | bytes 530432 | tf_op jit(solution)/shard_map/convert_element_type | solution.py:31
  19.3 0.3 fusion.17
  19.6 0.6 %slice-done = bf16[2,128,128]{2,1,0:T(8,128)(2,1)S(1)} async-done(((bf16[2,131,128]{2,1,0:T(8,128)(2,1)}), bf16[2,128,128]{2,1,0:T(8,128)(2,1)S(1)}, s32[]{:S(2)}) %slice-start) | async-done | bytes 65560 | tf_op jit(solution)/shard_map/slice | solution.py:101
  20.2 0.3 convolution_add_fusion.1
  20.4 0.6 %collective-permute-done.5 = bf16[2,131,256]{2,1,0:T(8,128)(2,1)S(1)} collective-permute-done((bf16[2,131,256]{2,1,0:T(8,128)(2,1)S(1)}, bf16[2,131,256]{2,1,0:T(8,128)(2,1)S(1)}, u32[]{:S(2)}, u32[]{:S(2)}) %collective-permute-start.5) | collective-permute-done | bytes 134176 | tf_op jit(solution)/shard_map/ppermute | solution.py:44
  21.0 2.0 %collective-permute-done.4 = bf16[2,131,256]{2,1,0:T(8,128)(2,1)S(1)} collective-permute-done((bf16[2,131,256]{2,1,0:T(8,128)(2,1)S(1)}, bf16[2,131,256]{2,1,0:T(8,128)(2,1)S(1)}, u32[]{:S(2)}, u32[]{:S(2)}) %collective-permute-start.4) | collective-permute-done | bytes 134176 | tf_op jit(solution)/shard_map/ppermute | solution.py:44
  23.2 6.5 %multiply_convert_fusion.5 = (bf16[256,512]{1,0:T(8,128)(2,1)S(1)}, bf16[256,512]{1,0:T(8,128)(2,1)S(1)}, bf16[256,512]{1,0:T(8,128)(2,1)S(1)}, bf16[256,512]{1,...) fusion(f32[256]{0:T(256)S(1)} %bitcast.77, f32[512]{0:T(512)S(1)} %bitcast.70, ...), kind=kLoop, calls=%fused_computation.26 | loop fusion | flops 3932160 | bytes 1583104 | tf_op jit(solution)/shard_map/convert_element_type | solution.py:31
  29.7 0.3 fusion.5
  30.0 0.3 fusion.9
  30.3 0.3 fusion.1
  30.8 0.1 copy.45
  30.9 0.1 copy.46
  31.0 0.1 pad_maximum_fusion.1
  31.2 1.2 %collective-permute-done.6 = f32[2,128,256]{2,1,0:T(8,128)S(1)} collective-permute-done((f32[2,128,256]{2,1,0:T(8,128)S(1)}, f32[2,128,256]{2,1,0:T(8,128)S(1)}, u32[]{:S(2)}, u32[]{:S(2)}) %collective-permute-start.6) | collective-permute-done | bytes 262176 | tf_op jit(solution)/shard_map/ppermute | solution.py:44
  32.4 0.6 %collective-permute-start.7 = (f32[2,128,128]{2,1,0:T(8,128)S(1)}, f32[2,128,128]{2,1,0:T(8,128)S(1)}, u32[]{:S(2)}, u32[]{:S(2)}) collective-permute-start(f32[2,128,128]{2,1,0:T(8,128)S(1)} %slice.250), channel_id=1, source_target_pairs={{0,2},{1,3},{2,0},{3,1},{4,6},{5,7},{6,4},{7,5},{8,10},{9,11},{10,... | collective-permute-start | bytes 393224 | tf_op jit(solution)/shard_map/ppermute | solution.py:44
  33.0 0.4 fusion.54
  33.4 4.6 %collective-permute-done.7 = f32[2,128,128]{2,1,0:T(8,128)S(1)} collective-permute-done((f32[2,128,128]{2,1,0:T(8,128)S(1)}, f32[2,128,128]{2,1,0:T(8,128)S(1)}, u32[]{:S(2)}, u32[]{:S(2)}) %collective-permute-start.7) | collective-permute-done | bytes 131104 | tf_op jit(solution)/shard_map/ppermute | solution.py:44
  38.1 0.7 %pad_maximum_fusion.4 = f32[2,128,128]{2,1,0:T(8,128)} fusion(f32[1,128,128]{2,1,0:T(8,128)S(1)} %get-tuple-element.10, f32[1,128,128]{2,1,0:T(8,128)S(1)} %get-tuple-element.9), kind=kLoop, calls=%fused_computation.52 | loop fusion | flops 32768 | bytes 262144 | tf_op jit(solution)/shard_map/stack | solution.py:151
  (55 shorter events, 0.9 us)
Async XLA Ops:
  1.7 11.7 %collective-permute-start.2 = (bf16[2,131,128]{2,1,0:T(8,128)(2,1)S(1)}, bf16[2,131,128]{2,1,0:T(8,128)(2,1)S(1)}, u32[]{:S(2)}, u32[]{:S(2)}) collective-permute-start(bf16[2,131,128]{2,1,0:T(8,128)(2,1)S(1)} %pad_maximum_fusion.5), channel_id=1, source_target_pairs={{0,16},{4,20},{8,24},{12,28},{16,0},{20,4},{24,8},{28,12},{1,17},{... | collective-permute-start | bytes 201224 | tf_op jit(solution)/shard_map/ppermute | solution.py:44
  5.9 0.7 %copy-start.4 = (s32[2,64]{1,0:T(2,128)S(1)}, s32[2,64]{1,0:T(2,128)}, u32[]{:S(2)}) copy-start(s32[2,64]{1,0:T(2,128)} %param.15) | copy-start | bytes 1540
  6.9 0.7 %copy-start.1 = (f32[2,128]{1,0:T(2,128)S(1)}, f32[2,128]{1,0:T(2,128)}, u32[]{:S(2)}) copy-start(f32[2,128]{1,0:T(2,128)} %param.10) | copy-start | bytes 3076
  6.9 23.9 %collective-permute-start.8 = (f32[2,128,64]{1,2,0:T(8,128)S(1)}, f32[2,128,64]{1,2,0:T(8,128)S(1)}, u32[]{:S(2)}, u32[]{:S(2)}) collective-permute-start(f32[2,128,64]{1,2,0:T(8,128)S(1)} %get-tuple-element.14), channel_id=1, source_target_pairs={{1,2},{3,4},{5,6},{7,8},{9,10},{11,12},{13,14},{15,16},{17,18},{19... | collective-permute-start | bytes 196616 | tf_op jit(solution)/shard_map/ppermute | solution.py:75
  7.8 3.0 %copy-start.2 = (f32[6,128]{1,0:T(8,128)S(1)}, f32[6,128]{1,0:T(8,128)}, u32[]{:S(2)}) copy-start(f32[6,128]{1,0:T(8,128)} %param.13) | copy-start | bytes 9220
  7.8 3.0 %copy-start.3 = (s32[6,128]{1,0:T(8,128)S(1)}, s32[6,128]{1,0:T(8,128)}, u32[]{:S(2)}) copy-start(s32[6,128]{1,0:T(8,128)} %param.14) | copy-start | bytes 9220
  7.8 3.9 %collective-permute-start = (f32[2,130,64]{1,2,0:T(8,128)S(1)}, f32[2,130,64]{1,2,0:T(8,128)S(1)}, u32[]{:S(2)}, u32[]{:S(2)}) collective-permute-start(f32[2,130,64]{1,2,0:T(8,128)S(1)} %pad_maximum_fusion.3), channel_id=1, source_target_pairs={{0,1},{1,0},{2,3},{3,2},{4,5},{5,4},{6,7},{7,6},{8,9},{9,8},{10,11... | collective-permute-start | bytes 199688 | tf_op jit(solution)/shard_map/ppermute | solution.py:44
  11.9 5.1 %collective-permute-start.1 = (f32[2,256]{1,0:T(2,128)S(1)}, f32[2,256]{1,0:T(2,128)S(1)}, u32[]{:S(2)}, u32[]{:S(2)}) collective-permute-start(f32[2,256]{1,0:T(2,128)S(1)} %get-tuple-element.38), channel_id=1, source_target_pairs={{0,2},{1,3},{2,0},{3,1},{4,6},{5,7},{6,4},{7,5},{8,10},{9,11},{10,... | collective-permute-start | bytes 6152 | tf_op jit(solution)/shard_map/ppermute | solution.py:44
  13.4 3.6 %copy-start = (bf16[2,131,128]{2,1,0:T(8,128)(2,1)}, bf16[2,131,128]{2,1,0:T(8,128)(2,1)S(1)}, u32[]{:S(2)}) copy-start(bf16[2,131,128]{2,1,0:T(8,128)(2,1)S(1)} %collective-permute-done.2) | copy-start | bytes 201220
  13.5 7.6 %collective-permute-start.5 = (bf16[2,131,256]{2,1,0:T(8,128)(2,1)S(1)}, bf16[2,131,256]{2,1,0:T(8,128)(2,1)S(1)}, u32[]{:S(2)}, u32[]{:S(2)}) collective-permute-start(bf16[2,131,256]{2,1,0:T(8,128)(2,1)S(1)} %pad_maximum_fusion.2), channel_id=1, source_target_pairs={{0,12},{4,8},{8,4},{12,0},{16,28},{20,24},{24,20},{28,16},{1,13},{... | collective-permute-start | bytes 402440 | tf_op jit(solution)/shard_map/ppermute | solution.py:44
  14.8 8.2 %collective-permute-start.4 = (bf16[2,131,256]{2,1,0:T(8,128)(2,1)S(1)}, bf16[2,131,256]{2,1,0:T(8,128)(2,1)S(1)}, u32[]{:S(2)}, u32[]{:S(2)}) collective-permute-start(bf16[2,131,256]{2,1,0:T(8,128)(2,1)S(1)} %pad_maximum_fusion.2), channel_id=1, source_target_pairs={{0,4},{4,0},{8,12},{12,8},{16,20},{20,16},{24,28},{28,24},{1,5},{5... | collective-permute-start | bytes 402440 | tf_op jit(solution)/shard_map/ppermute | solution.py:44
  16.6 6.6 %collective-permute-start.3 = (bf16[2,131,256]{2,1,0:T(8,128)(2,1)S(1)}, bf16[2,131,256]{2,1,0:T(8,128)(2,1)S(1)}, u32[]{:S(2)}, u32[]{:S(2)}) collective-permute-start(bf16[2,131,256]{2,1,0:T(8,128)(2,1)S(1)} %pad_maximum_fusion.2), channel_id=1, source_target_pairs={{0,8},{4,12},{8,0},{12,4},{16,24},{20,28},{24,16},{28,20},{1,9},{5... | collective-permute-start | bytes 402440 | tf_op jit(solution)/shard_map/ppermute | solution.py:44
  19.3 0.8 %slice-start = ((bf16[2,131,128]{2,1,0:T(8,128)(2,1)}), bf16[2,128,128]{2,1,0:T(8,128)(2,1)S(1)}, s32[]{:S(2)}) async-start(bf16[2,131,128]{2,1,0:T(8,128)(2,1)} %copy-done), calls=%async_computation | async-start | bytes 131072 | tf_op jit(solution)/shard_map/slice | solution.py:101
  30.7 1.6 %collective-permute-start.6 = (f32[2,128,256]{2,1,0:T(8,128)S(1)}, f32[2,128,256]{2,1,0:T(8,128)S(1)}, u32[]{:S(2)}, u32[]{:S(2)}) collective-permute-start(f32[2,128,256]{2,1,0:T(8,128)S(1)} %pad_maximum_fusion), channel_id=1, source_target_pairs={{0,1},{1,0},{2,3},{3,2},{4,5},{5,4},{6,7},{7,6},{8,9},{9,8},{10,11... | collective-permute-start | bytes 786440 | tf_op jit(solution)/shard_map/ppermute | solution.py:44
  32.4 5.6 %collective-permute-start.7 = (f32[2,128,128]{2,1,0:T(8,128)S(1)}, f32[2,128,128]{2,1,0:T(8,128)S(1)}, u32[]{:S(2)}, u32[]{:S(2)}) collective-permute-start(f32[2,128,128]{2,1,0:T(8,128)S(1)} %slice.250), channel_id=1, source_target_pairs={{0,2},{1,3},{2,0},{3,1},{4,6},{5,7},{6,4},{7,5},{8,10},{9,11},{10,... | collective-permute-start | bytes 393224 | tf_op jit(solution)/shard_map/ppermute | solution.py:44
  33.4 4.6 %copy-start.5 = (f32[128]{0:T(128)S(1)}, f32[128]{0:T(128)}, u32[]{:S(2)}) copy-start(f32[128]{0:T(128)} %param.12) | copy-start | bytes 1540
  33.4 4.6 %copy-start.6 = (f32[128]{0:T(128)S(1)}, f32[128]{0:T(128)}, u32[]{:S(2)}) copy-start(f32[128]{0:T(128)} %param.11) | copy-start | bytes 1540
